TPU v7x, 128 devices: a whole 4x4x4 slice. The times are simulated.
128 devices in a mesh: pos: 8 (over y, core), stream: 16 (over z, x).
Axes of the slice: x: 4, y: 4, z: 4, core: 2. Of those that a mesh axis runs over, the one named last changes fastest.
Arguments:
- tokens_in: bfloat16 [16, 4096, 8192], P('stream', 'pos'), may hold values from -6 to 6
- proj_in: bfloat16 [16, 4096, 256], P('stream', 'pos'), may hold values from -1.75 to 1.75
- step_raw: bfloat16 [16, 4096, 128], P('stream', 'pos')
- decay_log: float32 [128], replicated, may hold values from -0.7 to 0.7
- head_skip_weight: float32 [128], replicated, may hold values from 0.5 to 1.5
- row_counts: int32 [8, 16, 16], replicated, may hold values from 16 to 48, as said below
Outputs:
- layer_out: bfloat16 [16, 4096, 8192], P('stream', 'pos')
Inputs may be any that keep to these rules, and one draw needn't show every extreme that they name: For each p, every row and every column of row_counts[p] sums to 512; all rows and columns of row_counts[p] hold the same list of values in some order, and the list splits into pairs whose sum is twice the list's mean; each row_counts[p] holds the value 48.
All inputs are finite; a program needn't handle non-finite values.
Results may differ from a plain program's by a relative error of at most 0.0037.
Values may be sent and summed in bfloat16 or wider, within the bound.
No kernel may reach another device: no remote copies, remote signals or barrier semaphores. Data moves between devices by JAX's collectives and lax.ppermute only.
A program may use at most 256 MiB of HBM per device.

v0:
```python
import math

import jax
import jax.numpy as jnp
from jax import lax
from jax.sharding import PartitionSpec as P

BLOCK = 512


def entering(array, axis, combine, identity):
    peers, here = (lax.axis_size(axis), lax.axis_index(axis))
    everything = jax.tree.map(lambda part: lax.all_gather(part, axis), array)
    start = jax.tree.map(
        lambda part, zero: jnp.broadcast_to(jnp.asarray(zero, part.dtype), part.shape),
        array,
        identity,
    )

    def step(k, before):
        reached = k < here
        new = combine(before, jax.tree.map(lambda part: part[k], everything))
        return jax.tree.map(lambda a, b: jnp.where(reached, a, b), new, before)

    return lax.fori_loop(0, peers, step, start)


def block_parts(tokens, input_projections, steps_raw, decay_rates):
    length = tokens.shape[0]
    head_count = tokens.shape[1]
    state_size = input_projections.shape[1] // 2
    inputs = input_projections[:, :state_size]
    readout = input_projections[:, state_size:]
    discretization_deltas = jax.nn.softplus(steps_raw.astype(jnp.float32))
    cumulated = jnp.cumsum(discretization_deltas * decay_rates[None, :], axis=0)
    scores = jnp.dot(readout, inputs.T, preferred_element_type=jnp.float32)
    causal = (
        jnp.arange(length, dtype=jnp.int32)[:, None] >= jnp.arange(length, dtype=jnp.int32)[None, :]
    )
    group_size = math.gcd(head_count, 16)

    def one_group(first_head):
        cum_group = lax.dynamic_slice_in_dim(cumulated, first_head, group_size, 1)
        step_group = lax.dynamic_slice_in_dim(discretization_deltas, first_head, group_size, 1)
        token_group = lax.dynamic_slice_in_dim(tokens, first_head, group_size, 1)
        log_decay = jnp.where(
            causal[:, :, None], cum_group[:, None, :] - cum_group[None, :, :], -jnp.inf
        )
        weights = (scores[:, :, None] * jnp.exp(log_decay) * step_group[None, :, :]).astype(
            jnp.bfloat16
        )
        return jnp.einsum("tsh,shp->thp", weights, token_group, preferred_element_type=jnp.float32)

    first_heads = jnp.arange(head_count // group_size, dtype=jnp.int32) * group_size
    local_part = lax.map(one_group, first_heads)
    local_part = jnp.moveaxis(local_part, 0, 1).reshape(length, head_count, tokens.shape[2])
    ending = cumulated[-1]
    scaled = (
        (jnp.exp(ending[None, :] - cumulated) * discretization_deltas)[:, :, None] * tokens
    ).astype(jnp.bfloat16)
    carried = jnp.einsum("sn,shp->hnp", inputs, scaled, preferred_element_type=jnp.float32)
    return (local_part, cumulated, carried, jnp.exp(ending))


def block_output(local_part, cumulated, readout, tokens, head_skip_weight, carry_state):
    readable = carry_state.astype(jnp.bfloat16)
    inherited = jnp.einsum("tn,hnp->thp", readout, readable, preferred_element_type=jnp.float32)
    total = (
        local_part
        + jnp.exp(cumulated)[:, :, None] * inherited
        + head_skip_weight[None, :, None] * tokens.astype(jnp.float32)
    )
    return total.astype(jnp.bfloat16)


def combine_states(earlier, later):
    return (earlier[0] * later[0], later[0][:, None, None] * earlier[1] + later[1])


def on_device(tokens_in, proj_in, step_raw, decay_log, head_skip_weight, row_counts):
    stream_count = lax.axis_size("stream")
    stream_index = lax.axis_index("stream")
    place_index = lax.axis_index("pos")
    tokens = tokens_in[0]
    input_projections = proj_in[0]
    steps_raw = step_raw[0]
    local_rows = tokens.shape[0]
    inner_width = tokens.shape[1]
    head_count = steps_raw.shape[1]
    head_size = inner_width // head_count
    state_size = input_projections.shape[1] // 2
    capacity = 3 * local_rows // (2 * stream_count)
    decay_rates = -jnp.exp(decay_log)
    place_counts = lax.dynamic_index_in_dim(row_counts, place_index, 0, keepdims=False)
    send_counts = lax.dynamic_index_in_dim(place_counts, stream_index, 0, keepdims=False)
    recv_counts = lax.dynamic_index_in_dim(place_counts, stream_index, 1, keepdims=False)
    send_start = jnp.cumsum(send_counts) - send_counts
    slot_range = jnp.arange(capacity, dtype=jnp.int32)
    pick_rows = jnp.clip(send_start[:, None] + slot_range[None, :], 0, local_rows - 1).reshape(-1)
    send_tokens = jnp.take(tokens, pick_rows, axis=0).reshape(stream_count, capacity, inner_width)
    send_proj = jnp.take(input_projections, pick_rows, axis=0).reshape(
        stream_count, capacity, 2 * state_size
    )
    send_steps = jnp.take(steps_raw, pick_rows, axis=0).reshape(stream_count, capacity, head_count)
    arrived = (
        lax.all_to_all(send_tokens, "stream", split_axis=0, concat_axis=0, tiled=True),
        lax.all_to_all(send_proj, "stream", split_axis=0, concat_axis=0, tiled=True),
        lax.all_to_all(send_steps, "stream", split_axis=0, concat_axis=0, tiled=True),
    )
    recv_end = jnp.cumsum(recv_counts)
    recv_start = recv_end - recv_counts
    positions = jnp.arange(local_rows, dtype=jnp.int32)
    source = jnp.sum((recv_end[:, None] <= positions[None, :]).astype(jnp.int32), axis=0)
    chosen = (source[None, :] == jnp.arange(stream_count, dtype=jnp.int32)[:, None]).astype(
        jnp.int32
    )
    source_start = jnp.sum(chosen * recv_start[:, None], axis=0)
    flat_rows = source * capacity + positions - source_start
    ordered_tokens = jnp.take(
        arrived[0].reshape(stream_count * capacity, inner_width), flat_rows, axis=0
    )
    ordered_proj = jnp.take(
        arrived[1].reshape(stream_count * capacity, 2 * state_size), flat_rows, axis=0
    )
    ordered_steps = jnp.take(
        arrived[2].reshape(stream_count * capacity, head_count), flat_rows, axis=0
    )
    token_heads = ordered_tokens.reshape(local_rows, head_count, head_size)
    accumulated_attenuation = jnp.ones((head_count,), jnp.float32)
    total_state = jnp.zeros((head_count, state_size, head_size), jnp.float32)
    part_data = block_parts(token_heads, ordered_proj, ordered_steps, decay_rates)
    total_state = part_data[3][:, None, None] * total_state + part_data[2]
    accumulated_attenuation = accumulated_attenuation * part_data[3]
    incoming = entering(
        (accumulated_attenuation, total_state),
        "pos",
        combine_states,
        (jnp.ones_like(accumulated_attenuation), jnp.zeros_like(total_state)),
    )
    carry_state = incoming[1]
    pieces = block_output(
        part_data[0],
        part_data[1],
        ordered_proj[0:BLOCK, state_size:],
        token_heads,
        head_skip_weight,
        carry_state,
    )
    result = pieces.reshape(local_rows, inner_width)
    return result[None]


def solution(mesh):
    in_specs = (
        P("stream", "pos", None),
        P("stream", "pos", None),
        P("stream", "pos", None),
        P(),
        P(),
        P(),
    )
    out_specs = P("stream", "pos", None)
    return jax.shard_map(
        on_device, mesh=mesh, in_specs=in_specs, out_specs=out_specs, check_vma=False
    )
```

profile of v0, /device:TPU:1, one launch (start us, length us, event | category | flops | bytes accessed | tf_op | source)
XLA Modules:
  0.0 697.6 jit_solution(2473611532757443939)
XLA Ops:
  11.9 8.4 %all-to-all-start.2 = ((bf16[16,48,128]{2,1,0:T(8,128)(2,1)}), bf16[16,48,128]{2,1,0:T(8,128)(2,1)S(1)}, u32[]{:S(2)}, u32[]{:S(2)}) async-start(bf16[16,48,128]{2,1,0:T(8,128)(2,1)} %broadcast_select_fusion.3), calls=%async_computation.2 | async-start | bytes 393216 | tf_op jit(solution)/shard_map/all_to_all | solution.py:108
  23.0 26.4 %gather_fusion = bf16[768,8192]{1,0:T(8,128)(2,1)} fusion(bf16[512,8192]{1,0:T(8,128)(2,1)} %bitcast.95, s32[1024]{0:T(1024)S(1)} %pad_clamp_fusion.1), kind=kCustom, calls=%fused_computation | custom fusion | bytes 25168896 | tf_op jit(solution)/shard_map/jit(_take)/gather | solution.py:100
  50.3 6.7 all-to-all-start.1
  57.0 10.8 %broadcast_select_fusion = bf16[16,48,8192]{2,1,0:T(8,128)(2,1)} fusion(bf16[16,48,8192]{2,1,0:T(8,128)(2,1)} %bitcast.96, pred[16,48]{1,0:T(8,128)(4,1)S(1)} %compare_and_fusion), kind=kLoop, calls=%fused_computation.27 | loop fusion | flops 6291456 | bytes 25166592 | tf_op jit(solution)/shard_map/jit(_take)/select_n | solution.py:100
  67.8 6.8 all-to-all-start
  80.6 175.7 %all-to-all-done = bf16[16,48,8192]{2,1,0:T(8,128)(2,1)} async-done(((bf16[16,48,8192]{2,1,0:T(8,128)(2,1)}), bf16[16,48,8192]{2,1,0:T(8,128)(2,1)}, u32[]{:S(2)}, u32[]{:S(2)}) %all-to-all-start) | async-done | bytes 12582944 | tf_op jit(solution)/shard_map/all_to_all | solution.py:106
  256.2 21.7 %gather_fusion.1 = bf16[512,8192]{1,0:T(8,128)(2,1)} fusion(bf16[768,8192]{1,0:T(8,128)(2,1)} %bitcast.5, s32[1024]{0:T(1024)S(1)} %pad_clamp_fusion), kind=kCustom, calls=%fused_computation.1 | custom fusion | bytes 16779264 | tf_op jit(solution)/shard_map/jit(_take)/gather | solution.py:119
  278.0 12.3 %copy.52 = bf16[512,8192]{0,1:T(8,128)(2,1)} copy(bf16[512,8192]{1,0:T(8,128)(2,1)} %gather_fusion.1) | data formatting | bytes 16777216 | tf_op jit(solution)/shard_map/jit(_take)/gather | solution.py:119
  290.3 16.5 %copy_select_fusion = bf16[512,128,64]{0,1,2:T(8,128)(2,1)} fusion(bf16[512,128,64]{0,2,1:T(8,128)(2,1)} %bitcast.97, pred[512]{0:T(512)(128)(4,1)S(1)} %compare_and_fusion.1), kind=kLoop, calls=%fused_computation.29 | loop fusion | flops 4194304 | bytes 16777728 | tf_op jit(solution)/shard_map/jit(_take)/select_n | solution.py:119
  306.8 7.9 %add_bitcast_fusion = f32[128,128,64]{1,0,2:T(8,128)} fusion(f32[128]{0:T(128)S(1)} %exponential_multiply_fusion.1, bf16[512,128,64]{0,1,2:T(8,128)(2,1)} %copy_select_fusion, f32[512,128]{0,1:T(8,128)S(1)} %copy.61, bf16[512,256]{1,0:T(8,128)(2,1)S(1)} %broadcast_select_fusion.2), kind=kOutput, calls=%fused_computation.31 | convolution fusion | flops 1087373312 | bytes 12976640 | tf_op jit(solution)/shard_map/sn,shp->hnp/dot_general | solution.py:61
  315.2 13.5 %all-gather.1 = f32[8,1,128]{2,1,0:T(1,128)S(1)} all-gather(f32[1,1,128]{2,1,0:T(1,128)S(1)} %get-tuple-element.254), channel_id=1, replica_groups=mesh['pos'=8,'stream'=16] {'pos'}, dimensions={0}, use_global_device_ids=true | all-gather | bytes 4608 | tf_op jit(solution)/shard_map/all_gather | solution.py:13
  329.0 90.8 %while.25 = (s32[]{:T(128)}, f32[8,512,16,64]{1,3,2,0:T(8,128)}, s32[8]{0:T(128)S(1)}, bf16[512,128,64]{0,1,2:T(8,128)(2,1)}, f32[512,512]{1,0:T(8,128)S(1)}, /*...) while((s32[]{:T(128)}, f32[8,512,16,64]{1,3,2,0:T(8,128)}, ...), condition=%wide.region_7.8_spmd.clone, body=%wide.region_6.7_spmd.clone.sunk | while | flops 558104576 | bytes 7045287 | solution.py:55
  334.0 6.6 bitcast_dynamic-update-slice_fusion.2
  345.4 6.7 bitcast_dynamic-update-slice_fusion.2
  356.7 6.6 bitcast_dynamic-update-slice_fusion.2
  368.0 6.6 bitcast_dynamic-update-slice_fusion.2
  379.3 6.7 bitcast_dynamic-update-slice_fusion.2
  390.6 6.6 bitcast_dynamic-update-slice_fusion.2
  401.9 6.7 bitcast_dynamic-update-slice_fusion.2
  413.1 6.6 bitcast_dynamic-update-slice_fusion.2
  419.7 17.9 %copy.59 = f32[512,8,16,64]{0,2,1,3:T(8,128)} copy(f32[512,8,16,64]{0,3,2,1:T(8,128)} %bitcast.100) | data formatting | bytes 33554432 | tf_op jit(solution)/shard_map/transpose | solution.py:56
  437.6 36.6 %all-gather.4.cloned.1.call-done = f32[1024,128,64]{1,0,2:T(8,128)} async-done(((f32[128,128,64]{1,0,2:T(8,128)}), f32[1024,128,64]{1,0,2:T(8,128)}) %all-gather.4.cloned.1.call-update) | async-done | bytes 33554448 | tf_op jit(solution)/shard_map/all_gather | solution.py:13
  474.2 168.1 %while.26 = (s32[]{:T(128)}, f32[128,128,64]{2,1,0:T(8,128)}, s32[]{:T(128)}, f32[8,128]{1,0:T(8,128)S(1)}, f32[8,128,128,64]{2,1,0,3:T(8,128)}, /*index=5*/s32[]{:T(128)}, s32[]{:T(128)}) while((s32[]{:T(128)}, f32[128,128,64]{2,1,0:T(8,128)}, s32[]{:T(128)}, f32[8,128]{1,0:T(8,128)S(1)}, f32[8,128,128,64]{2,1,0,3:T(8,128)}, ...), condition=%wide.region_9.10_spmd.clone, body=%wide.region_8.9_spmd.clone.sunk | while | flops 4194308 | bytes 29361776 | solution.py:25
  478.8 6.9 copy.76
  485.7 6.0 fusion.41
  491.8 4.6 constant_dynamic-slice_fusion.10
  496.4 6.9 copy.76
  503.3 9.9 %fusion.41 = f32[128,128,64]{2,1,0:T(8,128)} fusion(f32[1,128,128,64]{3,2,1,0:T(8,128)} %copy.76, f32[128,128,64]{2,1,0:T(8,128)} %get-tuple-element.374, f32[128]{0:T(128)S(1)} %dynamic-slice_bitcast_fusion.3, pred[]{:T(512)S(6)} %compare.3, pred[]{:T(512)S(6)} %lt.120), kind=kLoop, calls=%fused_computation.18.clone.1 | loop fusion | flops 4194304 | bytes 12583426 | tf_op jit(solution)/shard_map/while/body/eval_jaxpr/jit(_where)/select_n | solution.py:23
  513.3 4.6 constant_dynamic-slice_fusion.10
  517.9 6.9 copy.76
  524.9 9.9 %fusion.41 = f32[128,128,64]{2,1,0:T(8,128)} fusion(f32[1,128,128,64]{3,2,1,0:T(8,128)} %copy.76, f32[128,128,64]{2,1,0:T(8,128)} %get-tuple-element.374, f32[128]{0:T(128)S(1)} %dynamic-slice_bitcast_fusion.3, pred[]{:T(512)S(6)} %compare.3, pred[]{:T(512)S(6)} %lt.120), kind=kLoop, calls=%fused_computation.18.clone.1 | loop fusion | flops 4194304 | bytes 12583426 | tf_op jit(solution)/shard_map/while/body/eval_jaxpr/jit(_where)/select_n | solution.py:23
  534.8 4.6 constant_dynamic-slice_fusion.10
  539.4 6.9 copy.76
  546.4 9.9 %fusion.41 = f32[128,128,64]{2,1,0:T(8,128)} fusion(f32[1,128,128,64]{3,2,1,0:T(8,128)} %copy.76, f32[128,128,64]{2,1,0:T(8,128)} %get-tuple-element.374, f32[128]{0:T(128)S(1)} %dynamic-slice_bitcast_fusion.3, pred[]{:T(512)S(6)} %compare.3, pred[]{:T(512)S(6)} %lt.120), kind=kLoop, calls=%fused_computation.18.clone.1 | loop fusion | flops 4194304 | bytes 12583426 | tf_op jit(solution)/shard_map/while/body/eval_jaxpr/jit(_where)/select_n | solution.py:23
  556.3 4.6 constant_dynamic-slice_fusion.10
  560.9 6.9 copy.76
  567.9 9.9 %fusion.41 = f32[128,128,64]{2,1,0:T(8,128)} fusion(f32[1,128,128,64]{3,2,1,0:T(8,128)} %copy.76, f32[128,128,64]{2,1,0:T(8,128)} %get-tuple-element.374, f32[128]{0:T(128)S(1)} %dynamic-slice_bitcast_fusion.3, pred[]{:T(512)S(6)} %compare.3, pred[]{:T(512)S(6)} %lt.120), kind=kLoop, calls=%fused_computation.18.clone.1 | loop fusion | flops 4194304 | bytes 12583426 | tf_op jit(solution)/shard_map/while/body/eval_jaxpr/jit(_where)/select_n | solution.py:23
  582.4 6.9 copy.76
  589.4 9.9 %fusion.41 = f32[128,128,64]{2,1,0:T(8,128)} fusion(f32[1,128,128,64]{3,2,1,0:T(8,128)} %copy.76, f32[128,128,64]{2,1,0:T(8,128)} %get-tuple-element.374, f32[128]{0:T(128)S(1)} %dynamic-slice_bitcast_fusion.3, pred[]{:T(512)S(6)} %compare.3, pred[]{:T(512)S(6)} %lt.120), kind=kLoop, calls=%fused_computation.18.clone.1 | loop fusion | flops 4194304 | bytes 12583426 | tf_op jit(solution)/shard_map/while/body/eval_jaxpr/jit(_where)/select_n | solution.py:23
  603.9 6.9 copy.76
  610.9 9.9 %fusion.41 = f32[128,128,64]{2,1,0:T(8,128)} fusion(f32[1,128,128,64]{3,2,1,0:T(8,128)} %copy.76, f32[128,128,64]{2,1,0:T(8,128)} %get-tuple-element.374, f32[128]{0:T(128)S(1)} %dynamic-slice_bitcast_fusion.3, pred[]{:T(512)S(6)} %compare.3, pred[]{:T(512)S(6)} %lt.120), kind=kLoop, calls=%fused_computation.18.clone.1 | loop fusion | flops 4194304 | bytes 12583426 | tf_op jit(solution)/shard_map/while/body/eval_jaxpr/jit(_where)/select_n | solution.py:23
  625.4 6.9 copy.76
  632.4 9.9 %fusion.41 = f32[128,128,64]{2,1,0:T(8,128)} fusion(f32[1,128,128,64]{3,2,1,0:T(8,128)} %copy.76, f32[128,128,64]{2,1,0:T(8,128)} %get-tuple-element.374, f32[128]{0:T(128)S(1)} %dynamic-slice_bitcast_fusion.3, pred[]{:T(512)S(6)} %compare.3, pred[]{:T(512)S(6)} %lt.120), kind=kLoop, calls=%fused_computation.18.clone.1 | loop fusion | flops 4194304 | bytes 12583426 | tf_op jit(solution)/shard_map/while/body/eval_jaxpr/jit(_where)/select_n | solution.py:23
  642.3 6.4 convert_element_type.35
  648.7 4.8 copy.63
  653.6 13.7 %fusion.9 = bf16[512,128,64]{0,1,2:T(8,128)(2,1)} fusion(bf16[512,128,64]{0,1,2:T(8,128)(2,1)} %get-tuple-element.388, f32[512,8,16,64]{0,2,1,3:T(8,128)} %copy.59, bf16[128,128,64]{1,0,2:T(8,128)(2,1)S(1)} %copy.63, f32[128]{0:T(128)S(1)} %copy-done.2, f32[512,128]{0,1:T(8,128)S(1)} %copy.60, bf16[512,256]{1,0:T(8,128)(2,1)S(1)} %broadcast_select_fusion.2), kind=kOutput, calls=%fused_computation.25 | convolution fusion | flops 1098907648 | bytes 36045312 | tf_op jit(solution)/shard_map/tn,hnp->thp/dot_general | solution.py:67
  667.2 11.3 %copy.64 = bf16[512,128,64]{0,2,1:T(8,128)(2,1)} copy(bf16[512,128,64]{0,1,2:T(8,128)(2,1)} %fusion.9) | data formatting | bytes 16777216 | tf_op jit(solution)/shard_map/convert_element_type | solution.py:73
  678.6 12.0 %copy.65 = bf16[1,512,8192]{2,1,0:T(8,128)(2,1)} copy(bf16[1,512,8192]{1,2,0:T(8,128)(2,1)} %bitcast.98) | data formatting | bytes 16777216 | tf_op jit(solution)/shard_map/broadcast_in_dim;reshape | solution.py:150
  (103 shorter events, 55.1 us)
Async XLA Ops:
  6.5 13.8 %copy-start = (bf16[1,512,256]{2,1,0:T(8,128)(2,1)S(1)}, bf16[1,512,256]{2,1,0:T(8,128)(2,1)}, u32[]{:S(2)}) copy-start(bf16[1,512,256]{2,1,0:T(8,128)(2,1)} %param.11) | copy-start | bytes 786436
  11.9 38.5 %all-to-all-start.2 = ((bf16[16,48,128]{2,1,0:T(8,128)(2,1)}), bf16[16,48,128]{2,1,0:T(8,128)(2,1)S(1)}, u32[]{:S(2)}, u32[]{:S(2)}) async-start(bf16[16,48,128]{2,1,0:T(8,128)(2,1)} %broadcast_select_fusion.3), calls=%async_computation.2 | async-start | bytes 393216 | tf_op jit(solution)/shard_map/all_to_all | solution.py:108
  50.3 17.4 %all-to-all-start.1 = ((bf16[16,48,256]{2,1,0:T(8,128)(2,1)}), bf16[16,48,256]{2,1,0:T(8,128)(2,1)S(1)}, u32[]{:S(2)}, u32[]{:S(2)}) async-start(bf16[16,48,256]{2,1,0:T(8,128)(2,1)} %broadcast_select_fusion.1), calls=%async_computation.1 | async-start | bytes 786432 | tf_op jit(solution)/shard_map/all_to_all | solution.py:107
  67.8 8.3 %copy-start.3 = (f32[128]{0:T(128)S(1)}, f32[128]{0:T(128)}, u32[]{:S(2)}) copy-start(f32[128]{0:T(128)} %param.13) | copy-start | bytes 1540
  67.8 188.5 %all-to-all-start = ((bf16[16,48,8192]{2,1,0:T(8,128)(2,1)}), bf16[16,48,8192]{2,1,0:T(8,128)(2,1)}, u32[]{:S(2)}, u32[]{:S(2)}) async-start(bf16[16,48,8192]{2,1,0:T(8,128)(2,1)} %broadcast_select_fusion), calls=%async_computation | async-start | bytes 25165824 | tf_op jit(solution)/shard_map/all_to_all | solution.py:106
  74.6 399.6 %all-gather.4.cloned.1.call-start = ((), (), s32[]{:S(2)}) async-start(), calls=%async_computation.3 | async-start | bytes 37748736 | tf_op jit(solution)/shard_map/all_gather | solution.py:13
  642.3 11.2 %copy-start.2 = (f32[128]{0:T(128)S(1)}, f32[128]{0:T(128)}, u32[]{:S(2)}) copy-start(f32[128]{0:T(128)} %param.14) | copy-start | bytes 1540
  678.6 12.0 %copy-start.1 = (bf16[1,512,256]{2,1,0:T(8,128)(2,1)S(1)}, bf16[1,512,256]{2,1,0:T(8,128)(2,1)}, u32[]{:S(2)}) copy-start(bf16[1,512,256]{2,1,0:T(8,128)(2,1)} %param.11) | copy-start | bytes 786436
Sparse Core Ops, SparseCore 0:
  314.8 159.3 all-gather.3
where the time goes:
time: 708 us; the launch traced here: 698 us
  local copies, waits for them, and re-layouts  230 us (32%)
  waiting for transfers between devices  212 us (30%)
  other arithmetic  114 us (16%)
  matrix products  75 us (11%)
  starting transfers between devices  22.1 us (3%)
  loops' own time  16.4 us (2%)
  between operations  13.9 us (2%)
  blocking collectives  13.5 us (2%)
    all_to_all x1, waiting for transfers between devices, on_device(): lax.all_to_all(send_tokens, 'stream', split_axis=0, concat_axis=0, tiled=...  176 us
    dynamic_slice x16, local copies, waits for them, and re-layouts, step(): new = combine(before, jax.tree.map(lambda part: part[k], everything))  92.4 us
    select_n x8, other arithmetic, step(): return jax.tree.map(lambda a, b: jnp.where(reached, a, b), new, before)  75.7 us
    dot_general x8, matrix products, one_group(): jnp.einsum('tsh,shp->thp', weights, token_group, preferred_element_type=j...  53.1 us
    all_gather x1, waiting for transfers between devices, entering(): everything = jax.tree.map(lambda part: lax.all_gather(part, axis), array)  36.6 us
    gather x2, local copies, waits for them, and re-layouts, on_device(): jnp.take(arrived[0].reshape(stream_count * capacity, inner_width), flat_r...  34 us
    gather x1, local copies, waits for them, and re-layouts, on_device(): jnp.take(tokens, pick_rows, axis=0)  26.4 us
    transpose x1, local copies, waits for them, and re-layouts, block_parts(): jnp.moveaxis(local_part, 0, 1).reshape(length, head_count, tokens.shape[2])  17.9 us
  transfers between devices with their start and end apart: 4, of which 2 were waited for; matrix products, arithmetic and copies ran while one was open for 20% of the time, Pallas kernels for 0%

commit v1 on v0

v1 whole, which is shorter than its diff:
```python
import functools

import jax
import jax.numpy as jnp
from jax import lax
from jax.experimental import pallas as pl
from jax.experimental.pallas import tpu as pltpu
from jax.sharding import PartitionSpec as P

GROUP = 8
TILE = 128


def output_kernel(
    scores_ref, cumg_ref, cumt_ref, stept_ref, tok_ref, skip_ref, c_ref, rd_ref, out_ref
):
    length = scores_ref.shape[0]
    heads = cumt_ref.shape[0]
    lane_low = lax.broadcasted_iota(jnp.int32, (1, 128), 1) < 64
    for q in range(heads // 2):
        x = tok_ref[:, 128 * q : 128 * (q + 1)]
        readable = rd_ref[q]
        skip = skip_ref[:, 128 * q : 128 * (q + 1)]
        for i in range(length // TILE):
            r0 = i * TILE
            width = (i + 1) * TILE
            rows = lax.broadcasted_iota(jnp.int32, (TILE, width), 0) + r0
            cols = lax.broadcasted_iota(jnp.int32, (TILE, width), 1)
            causal = rows >= cols
            sc = scores_ref[r0 : r0 + TILE, 0:width]
            parts = []
            decays = []
            for j in range(2):
                h = 2 * q + j
                ct = cumg_ref[0, r0 : r0 + TILE, h : h + 1]
                cs = cumt_ref[h : h + 1, 0:width]
                st = stept_ref[h : h + 1, 0:width]
                w = jnp.where(causal, jnp.exp(ct - cs), 0.0)
                wb = ((sc * w) * st).astype(jnp.bfloat16)
                parts.append(jnp.dot(wb, x[0:width], preferred_element_type=jnp.float32))
                decays.append(jnp.exp(ct))
            local = jnp.where(lane_low, parts[0], parts[1])
            inherited = jnp.dot(
                c_ref[r0 : r0 + TILE, :], readable, preferred_element_type=jnp.float32
            )
            decay = jnp.where(lane_low, decays[0], decays[1])
            xt = x[r0 : r0 + TILE].astype(jnp.float32)
            total = local + decay * inherited + skip * xt
            out_ref[r0 : r0 + TILE, 128 * q : 128 * (q + 1)] = total.astype(out_ref.dtype)


def block_output(scores, cum, steps, tokens, skip_lanes, readout, readable):
    length, heads = cum.shape
    groups = heads // GROUP
    width = GROUP * (tokens.shape[1] // heads)
    cum_grouped = cum.reshape(length, groups, GROUP).transpose(1, 0, 2)
    return pl.pallas_call(
        output_kernel,
        grid=(groups,),
        in_specs=[
            pl.BlockSpec((length, length), lambda g: (0, 0)),
            pl.BlockSpec((1, length, GROUP), lambda g: (g, 0, 0)),
            pl.BlockSpec((GROUP, length), lambda g: (g, 0)),
            pl.BlockSpec((GROUP, length), lambda g: (g, 0)),
            pl.BlockSpec((length, width), lambda g: (0, g)),
            pl.BlockSpec((1, width), lambda g: (0, g)),
            pl.BlockSpec((length, readout.shape[1]), lambda g: (0, 0)),
            pl.BlockSpec((GROUP // 2, readable.shape[1], 128), lambda g: (g, 0, 0)),
        ],
        out_specs=pl.BlockSpec((length, width), lambda g: (0, g)),
        out_shape=jax.ShapeDtypeStruct(tokens.shape, jnp.bfloat16),
        compiler_params=pltpu.CompilerParams(dimension_semantics=("arbitrary",)),
    )(scores, cum_grouped, cum.T, steps.T, tokens, skip_lanes, readout, readable)


def deliver(rows, pick_rows, flat_rows, stream_count, capacity):
    width = rows.shape[1]
    send = jnp.take(rows, pick_rows, axis=0).reshape(stream_count, capacity, width)
    arrived = lax.all_to_all(send, "stream", split_axis=0, concat_axis=0, tiled=True)
    return jnp.take(arrived.reshape(stream_count * capacity, width), flat_rows, axis=0)


def on_device(tokens_in, proj_in, step_raw, decay_log, head_skip_weight, row_counts):
    stream_count = lax.axis_size("stream")
    stream_index = lax.axis_index("stream")
    place_count = lax.axis_size("pos")
    place_index = lax.axis_index("pos")
    tokens = tokens_in[0]
    local_rows = tokens.shape[0]
    head_count = step_raw.shape[2]
    head_size = tokens.shape[1] // head_count
    state_size = proj_in.shape[2] // 2
    capacity = 3 * local_rows // (2 * stream_count)

    place_counts = lax.dynamic_index_in_dim(row_counts, place_index, 0, keepdims=False)
    send_counts = lax.dynamic_index_in_dim(place_counts, stream_index, 0, keepdims=False)
    recv_counts = lax.dynamic_index_in_dim(place_counts, stream_index, 1, keepdims=False)
    send_start = jnp.cumsum(send_counts) - send_counts
    slot_range = jnp.arange(capacity, dtype=jnp.int32)
    pick_rows = jnp.clip(send_start[:, None] + slot_range[None, :], 0, local_rows - 1).reshape(-1)
    recv_end = jnp.cumsum(recv_counts)
    recv_start = recv_end - recv_counts
    positions = jnp.arange(local_rows, dtype=jnp.int32)
    source = jnp.sum((recv_end[:, None] <= positions[None, :]).astype(jnp.int32), axis=0)
    source_start = jnp.take(recv_start, jnp.clip(source, 0, stream_count - 1))
    flat_rows = source * capacity + positions - source_start

    ordered_tokens = deliver(tokens, pick_rows, flat_rows, stream_count, capacity)
    ordered_proj = deliver(proj_in[0], pick_rows, flat_rows, stream_count, capacity)
    ordered_steps = deliver(step_raw[0], pick_rows, flat_rows, stream_count, capacity)

    inputs = ordered_proj[:, :state_size]
    readout = ordered_proj[:, state_size:]
    decay_rates = -jnp.exp(decay_log)
    steps = jax.nn.softplus(ordered_steps.astype(jnp.float32))
    cum = jnp.cumsum(steps * decay_rates[None, :], axis=0)
    ending = cum[-1]
    scale = jnp.exp(ending[None, :] - cum) * steps
    pairs = head_count // 2
    scaled = (scale[:, :, None] * ordered_tokens.reshape(local_rows, head_count, head_size)).astype(
        jnp.bfloat16
    )
    scaled = scaled.reshape(local_rows, pairs, 2 * head_size)
    carried = jnp.einsum("sn,sqc->qnc", inputs, scaled, preferred_element_type=jnp.float32)

    block_decay = jnp.exp(ending)
    all_decay = lax.all_gather(block_decay, "pos")
    all_carried = lax.all_gather(carried, "pos")
    earlier = jnp.arange(place_count, dtype=jnp.int32)
    between = (earlier[None, :] > earlier[:, None]) & (earlier[None, :] < place_index)
    weight = jnp.prod(jnp.where(between[:, :, None], all_decay[None, :, :], 1.0), axis=1)
    weight = jnp.where((earlier < place_index)[:, None], weight, 0.0)
    lane_weight = jnp.repeat(weight, head_size, axis=1).reshape(place_count, pairs, 1, 2 * head_size)
    state = jnp.sum(lane_weight * all_carried, axis=0)
    readable = state.astype(jnp.bfloat16)

    scores = jnp.dot(readout, inputs.T, preferred_element_type=jnp.float32)
    skip_lanes = jnp.repeat(head_skip_weight, head_size).reshape(1, -1)
    result = block_output(scores, cum, steps, ordered_tokens, skip_lanes, readout, readable)
    return result[None]


def solution(mesh):
    in_specs = (
        P("stream", "pos", None),
        P("stream", "pos", None),
        P("stream", "pos", None),
        P(),
        P(),
        P(),
    )
    out_specs = P("stream", "pos", None)
    return jax.shard_map(
        on_device, mesh=mesh, in_specs=in_specs, out_specs=out_specs, check_vma=False
    )
```

time: 708 us -> 557 us (0.79); the launches traced: 698 us -> 555 us
  local copies, waits for them, and re-layouts: 230 us -> 118 us
  waiting for transfers between devices: 212 us -> 294 us
  matrix products: 75 us -> 5.63 us
  other arithmetic: 114 us -> 53.1 us
  Pallas kernels: 0 us -> 34.8 us
  loops' own time: 16.4 us -> 0 us
    dynamic_slice x40 -> x0, local copies, waits for them, and re-layouts: 113 us -> none  [the longest x16 92.4 us: step(): new = combine(before, jax.tree.map(lambda part: part[k], everything))]
    all_gather x1, waiting for transfers between devices: 36.6 us -> 130 us  [on_device(): all_carried = lax.all_gather(carried, 'pos')]
    select_n x15 -> x9, other arithmetic: 105 us -> 23.3 us  [the longest x4 12.6 us: deliver(): jnp.take(rows, pick_rows, axis=0).reshape(stream_count, capacity, width)]
    dot_general x11 -> x2, matrix products: 75 us -> 5.63 us  [the longest x1 4.27 us: on_device(): jnp.einsum('sn,sqc->qnc', inputs, scaled, preferred_element_type=jnp.floa...]
    pallas_call x0 -> x1, Pallas kernels: none -> 34.8 us  [block_output(): pl.pallas_call(output_kernel, grid=(groups,), in_specs=[pl.BlockSpec((len...]
    all_gather x0 -> x1, local copies, waits for them, and re-layouts: none -> 31 us  [on_device(): all_carried = lax.all_gather(carried, 'pos')]
    another operation x2 -> x0, loops' own time: 16.4 us -> none  [the longest x1 16.4 us: block_parts(): local_part = lax.map(one_group, first_heads)]
    convert_element_type x2 -> x0, local copies, waits for them, and re-layouts: 16.2 us -> none  [the longest x1 11.3 us: block_output(): return total.astype(jnp.bfloat16)]
  transfers between devices with their start and end apart: 4 -> 4, of which waited for: 2 -> 2; matrix products, arithmetic and copies ran while one was open for 20% -> 13% of each run, Pallas kernels for 0% -> 0%
where the time goes in v1:
time: 557 us; the launch traced here: 555 us
  waiting for transfers between devices  294 us (53%)
  local copies, waits for them, and re-layouts  118 us (21%)
  other arithmetic  53.1 us (10%)
  Pallas kernels  34.8 us (6%)
  starting transfers between devices  22.1 us (4%)
  between operations  13.7 us (2%)
  blocking collectives  13.5 us (2%)
  matrix products  5.63 us (1%)
    all_to_all x3, waiting for transfers between devices, deliver(): lax.all_to_all(send, 'stream', split_axis=0, concat_axis=0, tiled=True)  164 us
    all_gather x1, waiting for transfers between devices, on_device(): all_carried = lax.all_gather(carried, 'pos')  130 us
    gather x5, local copies, waits for them, and re-layouts, deliver(): jnp.take(arrived.reshape(stream_count * capacity, width), flat_rows, axis=0)  37.1 us
    pallas_call x1, Pallas kernels, block_output(): pl.pallas_call(output_kernel, grid=(groups,), in_specs=[pl.BlockSpec((len...  34.8 us
    gather x3, local copies, waits for them, and re-layouts, deliver(): jnp.take(rows, pick_rows, axis=0).reshape(stream_count, capacity, width)  31.6 us
    all_gather x1, local copies, waits for them, and re-layouts, on_device(): all_carried = lax.all_gather(carried, 'pos')  31 us
    all_to_all x3, starting transfers between devices, deliver(): lax.all_to_all(send, 'stream', split_axis=0, concat_axis=0, tiled=True)  21.9 us
    all_gather x1, blocking collectives, on_device(): all_decay = lax.all_gather(block_decay, 'pos')  13.5 us
  transfers between devices with their start and end apart: 4, of which 2 were waited for; matrix products, arithmetic and copies ran while one was open for 13% of the time, Pallas kernels for 0%

profile of v1, /device:TPU:1, one launch (start us, length us, event | category | flops | bytes accessed | tf_op | source)
XLA Modules:
  0.0 555.2 jit_solution(13440223844275733469)
XLA Ops:
  6.5 0.7 fusion.19
  7.4 0.1 reduce.11
  7.5 0.7 bitcast_subtract_fusion
  8.5 2.5 gather_fusion.2
  11.0 0.8 broadcast_select_fusion.4
  11.9 8.4 %all-to-all-start.1 = ((bf16[16,48,128]{2,1,0:T(8,128)(2,1)}), bf16[16,48,128]{2,1,0:T(8,128)(2,1)S(1)}, u32[]{:S(2)}, u32[]{:S(2)}) async-start(bf16[16,48,128]{2,1,0:T(8,128)(2,1)} %broadcast_select_fusion.4), calls=%async_computation.1 | async-start | bytes 393216 | tf_op jit(solution)/shard_map/all_to_all | solution.py:79
  20.3 26.4 %gather_fusion.4 = bf16[768,8192]{1,0:T(8,128)(2,1)} fusion(bf16[512,8192]{1,0:T(8,128)(2,1)} %bitcast.99, s32[1024]{0:T(1024)S(1)} %pad_clamp_fusion.1), kind=kCustom, calls=%fused_computation.4 | custom fusion | bytes 25168896 | tf_op jit(solution)/shard_map/jit(_take)/gather | solution.py:78
  46.7 2.6 gather_fusion
  49.4 0.9 broadcast_select_fusion.2
  50.3 6.7 %all-to-all-start = ((bf16[16,48,256]{2,1,0:T(8,128)(2,1)}), bf16[16,48,256]{2,1,0:T(8,128)(2,1)S(1)}, u32[]{:S(2)}, u32[]{:S(2)}) async-start(bf16[16,48,256]{2,1,0:T(8,128)(2,1)} %broadcast_select_fusion.2), calls=%async_computation | async-start | bytes 786432 | tf_op jit(solution)/shard_map/all_to_all | solution.py:79
  57.0 10.8 %broadcast_select_fusion = bf16[16,48,8192]{2,1,0:T(8,128)(2,1)} fusion(bf16[16,48,8192]{2,1,0:T(8,128)(2,1)} %bitcast.101, pred[16,48]{1,0:T(8,128)(4,1)S(1)} %compare_and_fusion), kind=kLoop, calls=%fused_computation.9 | loop fusion | flops 6291456 | bytes 25166592 | tf_op jit(solution)/shard_map/jit(_take)/select_n | solution.py:78
  67.8 6.8 %all-to-all-start.2 = ((bf16[16,48,8192]{2,1,0:T(8,128)(2,1)}), bf16[16,48,8192]{2,1,0:T(8,128)(2,1)}, u32[]{:S(2)}, u32[]{:S(2)}) async-start(bf16[16,48,8192]{2,1,0:T(8,128)(2,1)} %broadcast_select_fusion), calls=%async_computation.2 | async-start | bytes 25165824 | tf_op jit(solution)/shard_map/all_to_all | solution.py:79
  74.7 0.2 all-gather.4.cloned.1.call-start
  74.9 0.9 dynamic-slice_reduce_fusion
  75.8 0.1 reduce
  75.9 0.7 fusion.23
  76.7 4.5 compare_select_fusion.6
  81.3 5.5 compare_and_fusion.1
  86.8 1.3 gather_fusion.3
  88.2 0.1 copy.33
  88.3 0.9 compare_select_fusion.1
  89.3 0.2 copy.34
  89.4 0.1 fusion.24
  89.6 0.2 copy.35
  89.8 0.2 exponential_reduce_fusion
  90.0 0.2 fusion.11
  90.2 2.0 gather_fusion.1
  92.2 0.1 broadcast_select_fusion.3
  92.3 163.9 %all-to-all-done.2 = bf16[16,48,8192]{2,1,0:T(8,128)(2,1)} async-done(((bf16[16,48,8192]{2,1,0:T(8,128)(2,1)}), bf16[16,48,8192]{2,1,0:T(8,128)(2,1)}, u32[]{:S(2)}, u32[]{:S(2)}) %all-to-all-start.2) | async-done | bytes 12582944 | tf_op jit(solution)/shard_map/all_to_all | solution.py:79
  256.3 21.7 %gather_fusion.5 = bf16[512,8192]{1,0:T(8,128)(2,1)} fusion(bf16[768,8192]{1,0:T(8,128)(2,1)} %bitcast.37, s32[1024]{0:T(1024)S(1)} %pad_clamp_fusion), kind=kCustom, calls=%fused_computation.5 | custom fusion | bytes 16779264 | tf_op jit(solution)/shard_map/jit(_take)/gather | solution.py:80
  278.0 12.0 %copy.41 = bf16[512,8192]{0,1:T(8,128)(2,1)} copy(bf16[512,8192]{1,0:T(8,128)(2,1)} %gather_fusion.5) | data formatting | bytes 16777216 | tf_op jit(solution)/shard_map/jit(_take)/gather | solution.py:80
  289.9 2.1 mul.59
  292.1 5.7 %fusion = bf16[512,64,128]{0,2,1:T(8,128)(2,1)S(1)} fusion(bf16[512,64,128]{0,2,1:T(8,128)(2,1)} %bitcast.102, pred[512]{0:T(512)(128)(4,1)S(1)} %get-tuple-element.16, f32[512,64,128]{0,2,1:T(8,128)S(1)} %bitcast.100), kind=kLoop, calls=%fused_computation.8 | loop fusion | flops 16777216 | bytes 33554944 | tf_op jit(solution)/shard_map/convert_element_type | solution.py:120
  297.8 4.3 convolution_bitcast_fusion
  302.0 5.6 %copy.38 = f32[64,128,128]{2,1,0:T(8,128)} copy(f32[64,128,128]{1,2,0:T(8,128)} %convolution_bitcast_fusion) | data formatting | bytes 8388608 | tf_op jit(solution)/shard_map/sn,sqc->qnc/transpose | solution.py:124
  307.8 0.7 reshape_reshape.4.skip_ref
  308.5 13.5 %all-gather.1 = f32[8,1,128]{2,1,0:T(1,128)S(1)} all-gather(f32[1,1,128]{2,1,0:T(1,128)S(1)} %bitcast.124), channel_id=1, replica_groups=mesh['pos'=8,'stream'=16] {'pos'}, dimensions={0}, use_global_device_ids=true | all-gather | bytes 4608 | tf_op jit(solution)/shard_map/all_gather | solution.py:127
  322.2 0.2 broadcast_in_dim.145
  322.4 0.1 mul.56
  322.6 2.9 copy.36
  325.5 0.7 slice.49.c_ref
  326.1 1.4 fusion.14.scores_ref
  327.5 9.6 %broadcast_select_fusion.1.tok_ref = bf16[512,8192]{1,0:T(8,128)(2,1)} fusion(bf16[512,8192]{1,0:T(8,128)(2,1)} %gather_fusion.5, pred[512]{0:T(512)(128)(4,1)S(1)} %get-tuple-element.16), kind=kLoop, calls=%fused_computation.10 | loop fusion | flops 4194304 | bytes 16777728 | tf_op jit(solution)/shard_map/jit(_take)/select_n | solution.py:80
  337.1 130.1 %all-gather.4.cloned.1.call-done = f32[512,128,128]{2,1,0:T(8,128)} async-done(((f32[64,128,128]{2,1,0:T(8,128)}), f32[512,128,128]{2,1,0:T(8,128)}) %all-gather.4.cloned.1.call-update) | async-done | bytes 33554448 | tf_op jit(solution)/shard_map/all_gather | solution.py:128
  467.2 31.0 %copy.39 = f32[8,64,128,128]{2,3,1,0:T(8,128)} copy(f32[8,64,128,128]{3,2,1,0:T(8,128)} %bitcast.103) | data formatting | bytes 67108864 | tf_op jit(solution)/shard_map/all_gather | solution.py:128
  498.3 12.3 %multiply_reduce_fusion = bf16[64,128,128]{1,2,0:T(8,128)(2,1)S(1)} fusion(f32[8,64,128,128]{2,3,1,0:T(8,128)} %copy.39, f32[8,64,128]{2,1,0:T(8,128)S(1)} %mul.56), kind=kLoop, calls=%fused_computation.6 | loop fusion | flops 15728640 | bytes 35913728 | tf_op jit(solution)/shard_map/reduce_sum | solution.py:134
  510.6 2.9 copy.40.rd_ref
  513.5 34.8 %shard_map.64 = bf16[512,8192]{1,0:T(8,128)(2,1)} custom-call(f32[512,512]{1,0:T(8,128)} %fusion.14.scores_ref, f32[16,512,8]{2,1,0:T(8,128)} %bitcast.105, f32[128,512]{1,0:T(8,128)} %bitcast.110, f32[128,512]{1,0:T(8,128)} %get-tuple-element.23.stept_ref, bf16[512,8192]{1,0:T(8,128)(2,1)} %broadcast_select_fusion.1.tok_ref, ...), custom_call_target="tpu_custom_call" | custom-call | tf_op jit(solution)/shard_map/pallas_call | solution.py:57
  (40 shorter events, 1.1 us)
Async XLA Ops:
  6.5 40.2 %copy-start = (bf16[1,512,256]{2,1,0:T(8,128)(2,1)S(1)}, bf16[1,512,256]{2,1,0:T(8,128)(2,1)}, u32[]{:S(2)}) copy-start(bf16[1,512,256]{2,1,0:T(8,128)(2,1)} %param.7) | copy-start | bytes 786436
  11.9 38.5 %all-to-all-start.1 = ((bf16[16,48,128]{2,1,0:T(8,128)(2,1)}), bf16[16,48,128]{2,1,0:T(8,128)(2,1)S(1)}, u32[]{:S(2)}, u32[]{:S(2)}) async-start(bf16[16,48,128]{2,1,0:T(8,128)(2,1)} %broadcast_select_fusion.4), calls=%async_computation.1 | async-start | bytes 393216 | tf_op jit(solution)/shard_map/all_to_all | solution.py:79
  50.3 17.5 %all-to-all-start = ((bf16[16,48,256]{2,1,0:T(8,128)(2,1)}), bf16[16,48,256]{2,1,0:T(8,128)(2,1)S(1)}, u32[]{:S(2)}, u32[]{:S(2)}) async-start(bf16[16,48,256]{2,1,0:T(8,128)(2,1)} %broadcast_select_fusion.2), calls=%async_computation | async-start | bytes 786432 | tf_op jit(solution)/shard_map/all_to_all | solution.py:79
  67.8 19.0 %copy-start.4 = (f32[128]{0:T(128)S(1)}, f32[128]{0:T(128)}, u32[]{:S(2)}) copy-start(f32[128]{0:T(128)} %param.9) | copy-start | bytes 1540
  67.8 188.5 %all-to-all-start.2 = ((bf16[16,48,8192]{2,1,0:T(8,128)(2,1)}), bf16[16,48,8192]{2,1,0:T(8,128)(2,1)}, u32[]{:S(2)}, u32[]{:S(2)}) async-start(bf16[16,48,8192]{2,1,0:T(8,128)(2,1)} %broadcast_select_fusion), calls=%async_computation.2 | async-start | bytes 25165824 | tf_op jit(solution)/shard_map/all_to_all | solution.py:79
  74.7 392.6 %all-gather.4.cloned.1.call-start = ((), (), s32[]{:S(2)}) async-start(), calls=%async_computation.3 | async-start | bytes 37748736 | tf_op jit(solution)/shard_map/all_gather | solution.py:128
  89.8 232.7 %copy-start.2 = (f32[16,8,4,128]{3,1,2,0:T(8,128)}, f32[16,8,4,128]{3,1,2,0:T(8,128)S(1)}, u32[]{:S(2)}) copy-start(f32[16,8,4,128]{3,1,2,0:T(8,128)S(1)} %copy.50) | copy-start | bytes 786436
  302.0 5.7 %copy-start.3 = (f32[128]{0:T(128)S(1)}, f32[128]{0:T(128)}, u32[]{:S(2)}) copy-start(f32[128]{0:T(128)} %param.10) | copy-start | bytes 1540
  513.5 34.8 %copy-start.1 = (bf16[1,512,256]{2,1,0:T(8,128)(2,1)S(1)}, bf16[1,512,256]{2,1,0:T(8,128)(2,1)}, u32[]{:S(2)}) copy-start(bf16[1,512,256]{2,1,0:T(8,128)(2,1)} %param.7) | copy-start | bytes 786436
Sparse Core Ops, SparseCore 0:
  307.8 159.3 all-gather.3

commit v2 on v1

v2 whole, which is shorter than its diff:
```python
import jax
import jax.numpy as jnp
from jax import lax
from jax.experimental import pallas as pl
from jax.experimental.pallas import tpu as pltpu
from jax.sharding import PartitionSpec as P

GROUP = 8
TILE = 128
CHUNKS = 4
EXTRA = 8


def lane_pick(low, high):
    lane_low = lax.broadcasted_iota(jnp.int32, (1, 128), 1) < 64
    return jnp.where(lane_low, low, high)


def carried_kernel(bt_ref, facg_ref, decay_ref, tok_ref, out_ref):
    pairs = out_ref.shape[0]
    state_size = bt_ref.shape[0]
    for q in range(pairs):
        x = tok_ref[:, 128 * q : 128 * (q + 1)].astype(jnp.float32)
        factor = lane_pick(facg_ref[0, :, 2 * q : 2 * q + 1], facg_ref[0, :, 2 * q + 1 : 2 * q + 2])
        scaled = (factor * x).astype(jnp.bfloat16)
        out_ref[q, 0:state_size, :] = jnp.dot(
            bt_ref[...], scaled, preferred_element_type=jnp.float32
        )
        rows = lax.broadcasted_iota(jnp.int32, (EXTRA, 128), 0)
        decay = decay_ref[:, 128 * q : 128 * (q + 1)]
        out_ref[q, state_size : state_size + EXTRA, :] = jnp.where(rows == 0, decay, 0.0)


def local_kernel(scores_ref, cumg_ref, cumt_ref, stept_ref, tok_ref, skip_ref, out_ref):
    length = scores_ref.shape[0]
    heads = cumt_ref.shape[0]
    for q in range(heads // 2):
        x = tok_ref[:, 128 * q : 128 * (q + 1)]
        skip = skip_ref[:, 128 * q : 128 * (q + 1)]
        for i in range(length // TILE):
            r0 = i * TILE
            width = (i + 1) * TILE
            rows = lax.broadcasted_iota(jnp.int32, (TILE, width), 0) + r0
            cols = lax.broadcasted_iota(jnp.int32, (TILE, width), 1)
            causal = rows >= cols
            sc = scores_ref[r0 : r0 + TILE, 0:width]
            parts = []
            for j in range(2):
                h = 2 * q + j
                ct = cumg_ref[0, r0 : r0 + TILE, h : h + 1]
                cs = cumt_ref[h : h + 1, 0:width]
                st = stept_ref[h : h + 1, 0:width]
                w = jnp.where(causal, jnp.exp(ct - cs), 0.0)
                wb = ((sc * w) * st).astype(jnp.bfloat16)
                parts.append(jnp.dot(wb, x[0:width], preferred_element_type=jnp.float32))
            xt = x[r0 : r0 + TILE].astype(jnp.float32)
            total = lane_pick(parts[0], parts[1]) + skip * xt
            out_ref[r0 : r0 + TILE, 128 * q : 128 * (q + 1)] = total


def combine_kernel(place_ref, *refs):
    if len(refs) == 6:
        refs = refs[1:]
    part_ref, gath_ref, cumg_ref, c_ref, out_ref = refs
    here = place_ref[0]
    peers = gath_ref.shape[0]
    pairs = gath_ref.shape[1]
    state_size = c_ref.shape[1]
    for q in range(pairs):
        run = jnp.ones((1, 128), jnp.float32)
        state = jnp.zeros((state_size, 128), jnp.float32)
        for k in range(peers - 1, -1, -1):
            if k + 1 < peers:
                later = gath_ref[k + 1, q, state_size : state_size + 1, :]
                run = jnp.where(k + 1 < here, run * later, 1.0)
            weight = jnp.where(k < here, run, 0.0)
            state = state + weight * gath_ref[k, q, 0:state_size, :]
        readable = state.astype(jnp.bfloat16)
        inherited = jnp.dot(c_ref[...], readable, preferred_element_type=jnp.float32)
        decay = lane_pick(
            jnp.exp(cumg_ref[0, :, 2 * q : 2 * q + 1]), jnp.exp(cumg_ref[0, :, 2 * q + 1 : 2 * q + 2])
        )
        total = part_ref[:, 128 * q : 128 * (q + 1)] + decay * inherited
        out_ref[:, 128 * q : 128 * (q + 1)] = total.astype(out_ref.dtype)


def arbitrary():
    return pltpu.CompilerParams(dimension_semantics=("arbitrary",))


def carried_call(bt, fac_grouped, decay_lanes, tokens, first):
    length, width = tokens.shape
    groups = width // (GROUP * 64)
    state_size = bt.shape[0]
    return pl.pallas_call(
        carried_kernel,
        grid=(groups,),
        in_specs=[
            pl.BlockSpec(bt.shape, lambda g: (0, 0)),
            pl.BlockSpec((1, length, GROUP), lambda g: (g + first, 0, 0)),
            pl.BlockSpec((1, GROUP * 64), lambda g: (0, g + first)),
            pl.BlockSpec((length, GROUP * 64), lambda g: (0, g)),
        ],
        out_specs=pl.BlockSpec((GROUP // 2, state_size + EXTRA, 128), lambda g: (g, 0, 0)),
        out_shape=jax.ShapeDtypeStruct((width // 128, state_size + EXTRA, 128), jnp.float32),
        compiler_params=arbitrary(),
    )(bt, fac_grouped, decay_lanes, tokens)


def local_call(scores, cum_grouped, cum_t, step_t, tokens, skip_lanes, first):
    length, width = tokens.shape
    groups = width // (GROUP * 64)
    return pl.pallas_call(
        local_kernel,
        grid=(groups,),
        in_specs=[
            pl.BlockSpec((length, length), lambda g: (0, 0)),
            pl.BlockSpec((1, length, GROUP), lambda g: (g + first, 0, 0)),
            pl.BlockSpec((GROUP, length), lambda g: (g + first, 0)),
            pl.BlockSpec((GROUP, length), lambda g: (g + first, 0)),
            pl.BlockSpec((length, GROUP * 64), lambda g: (0, g)),
            pl.BlockSpec((1, GROUP * 64), lambda g: (0, g + first)),
        ],
        out_specs=pl.BlockSpec((length, GROUP * 64), lambda g: (0, g)),
        out_shape=jax.ShapeDtypeStruct((length, width), jnp.float32),
        compiler_params=arbitrary(),
    )(scores, cum_grouped, cum_t, step_t, tokens, skip_lanes)


def combine_call(buffer, place, partial, gathered, cum_grouped, readout, first, total_width):
    length, width = partial.shape
    groups = width // (GROUP * 64)
    state_rows = gathered.shape[2]
    in_specs = [
        pl.BlockSpec((length, GROUP * 64), lambda g: (0, g)),
        pl.BlockSpec((gathered.shape[0], GROUP // 2, state_rows, 128), lambda g: (0, g, 0, 0)),
        pl.BlockSpec((1, length, GROUP), lambda g: (g + first, 0, 0)),
        pl.BlockSpec(readout.shape, lambda g: (0, 0)),
    ]
    operands = [partial, gathered, cum_grouped, readout]
    aliases = {}
    if buffer is not None:
        in_specs = [pl.BlockSpec(memory_space=pl.ANY)] + in_specs
        operands = [buffer] + operands
        aliases = {1: 0}
    return pl.pallas_call(
        combine_kernel,
        grid=(groups,),
        in_specs=[pl.BlockSpec(memory_space=pltpu.SMEM)] + in_specs,
        out_specs=pl.BlockSpec((length, GROUP * 64), lambda g: (0, g + first)),
        out_shape=jax.ShapeDtypeStruct((length, total_width), jnp.bfloat16),
        input_output_aliases=aliases,
        compiler_params=arbitrary(),
    )(place, *operands)


def deliver(rows, pick_rows, flat_rows, stream_count, capacity):
    width = rows.shape[1]
    send = jnp.take(rows, pick_rows, axis=0, mode="clip").reshape(stream_count, capacity, width)
    arrived = lax.all_to_all(send, "stream", split_axis=0, concat_axis=0, tiled=True)
    return jnp.take(
        arrived.reshape(stream_count * capacity, width), flat_rows, axis=0, mode="clip"
    )


def on_device(tokens_in, proj_in, step_raw, decay_log, head_skip_weight, row_counts):
    stream_count = lax.axis_size("stream")
    stream_index = lax.axis_index("stream")
    place_index = lax.axis_index("pos")
    tokens = tokens_in[0]
    local_rows, inner = tokens.shape
    head_count = step_raw.shape[2]
    head_size = inner // head_count
    state_size = proj_in.shape[2] // 2
    capacity = 3 * local_rows // (2 * stream_count)

    place_counts = lax.dynamic_index_in_dim(row_counts, place_index, 0, keepdims=False)
    send_counts = lax.dynamic_index_in_dim(place_counts, stream_index, 0, keepdims=False)
    recv_counts = lax.dynamic_index_in_dim(place_counts, stream_index, 1, keepdims=False)
    send_start = jnp.cumsum(send_counts) - send_counts
    slot_range = jnp.arange(capacity, dtype=jnp.int32)
    pick_rows = jnp.clip(send_start[:, None] + slot_range[None, :], 0, local_rows - 1).reshape(-1)
    recv_end = jnp.cumsum(recv_counts)
    recv_start = recv_end - recv_counts
    positions = jnp.arange(local_rows, dtype=jnp.int32)
    source = jnp.sum((recv_end[:, None] <= positions[None, :]).astype(jnp.int32), axis=0)
    source = jnp.clip(source, 0, stream_count - 1)
    source_start = jnp.take(recv_start, source)
    flat_rows = source * capacity + positions - source_start

    ordered_proj = deliver(proj_in[0], pick_rows, flat_rows, stream_count, capacity)
    ordered_steps = deliver(step_raw[0], pick_rows, flat_rows, stream_count, capacity)

    inputs = ordered_proj[:, :state_size]
    readout = ordered_proj[:, state_size:]
    decay_rates = -jnp.exp(decay_log)
    steps = jax.nn.softplus(ordered_steps.astype(jnp.float32))
    cum = jnp.cumsum(steps * decay_rates[None, :], axis=0)
    ending = cum[-1]
    factor = jnp.exp(ending[None, :] - cum) * steps
    groups = head_count // GROUP

    def grouped(a):
        return a.reshape(local_rows, groups, GROUP).transpose(1, 0, 2)

    cum_grouped = grouped(cum)
    fac_grouped = grouped(factor)
    cum_t = cum.T
    step_t = steps.T
    decay_lanes = jnp.repeat(jnp.exp(ending), head_size).reshape(1, -1)
    skip_lanes = jnp.repeat(head_skip_weight, head_size).reshape(1, -1)
    scores = jnp.dot(readout, inputs.T, preferred_element_type=jnp.float32)
    bt = inputs.T
    place = place_index.astype(jnp.int32).reshape(1)

    width = inner // CHUNKS
    groups_per_chunk = groups // CHUNKS
    pieces = []
    for c in range(CHUNKS):
        chunk_tokens = deliver(
            tokens[:, c * width : (c + 1) * width], pick_rows, flat_rows, stream_count, capacity
        )
        first = c * groups_per_chunk
        carried = carried_call(bt, fac_grouped, decay_lanes, chunk_tokens, first)
        gathered = lax.all_gather(carried, "pos")
        partial = local_call(scores, cum_grouped, cum_t, step_t, chunk_tokens, skip_lanes, first)
        pieces.append((partial, gathered, first))
    result = None
    for partial, gathered, first in pieces:
        result = combine_call(
            result, place, partial, gathered, cum_grouped, readout, first, inner
        )
    return result[None]


def solution(mesh):
    in_specs = (
        P("stream", "pos", None),
        P("stream", "pos", None),
        P("stream", "pos", None),
        P(),
        P(),
        P(),
    )
    out_specs = P("stream", "pos", None)
    return jax.shard_map(
        on_device, mesh=mesh, in_specs=in_specs, out_specs=out_specs, check_vma=False
    )
```

time: 557 us -> 395 us (0.71)
  the two profiles are of different devices: /device:TPU:1 before, /device:TPU:24 now
where the time goes in v2:
time: 395 us; the launch traced here: 390 us
  blocking collectives  138 us (35%)
  Pallas kernels  91.7 us (23%)
  local copies, waits for them, and re-layouts  88.4 us (22%)
  waiting for transfers between devices  26.3 us (7%)
  starting transfers between devices  19.1 us (5%)
  between operations  13.5 us (3%)
  other arithmetic  12.5 us (3%)
    all_to_all x3, blocking collectives, deliver(): lax.all_to_all(send, 'stream', split_axis=0, concat_axis=0, tiled=True)  138 us
    pallas_call x4, Pallas kernels, local_call(): pl.pallas_call(local_kernel, grid=(groups,), in_specs=[pl.BlockSpec((leng...  38 us
    gather x6, local copies, waits for them, and re-layouts, deliver(): jnp.take(rows, pick_rows, axis=0, mode='clip')  37.7 us
    gather x7, local copies, waits for them, and re-layouts, deliver(): jnp.take(arrived.reshape(stream_count * capacity, width), flat_rows, axis...  33.6 us
    pallas_call x4, Pallas kernels, combine_call(): pl.pallas_call(combine_kernel, grid=(groups,), in_specs=[pl.BlockSpec(mem...  30.9 us
    all_to_all x3, waiting for transfers between devices, deliver(): lax.all_to_all(send, 'stream', split_axis=0, concat_axis=0, tiled=True)  26.2 us
    pallas_call x4, Pallas kernels, carried_call(): pl.pallas_call(carried_kernel, grid=(groups,), in_specs=[pl.BlockSpec(bt....  22.8 us
    all_to_all x3, starting transfers between devices, deliver(): lax.all_to_all(send, 'stream', split_axis=0, concat_axis=0, tiled=True)  18.6 us
  transfers between devices with their start and end apart: 7, of which 2 were waited for; matrix products, arithmetic and copies ran while one was open for 23% of the time, Pallas kernels for 20%

profile of v2, /device:TPU:24, one launch (start us, length us, event | category | flops | bytes accessed | tf_op | source)
XLA Modules:
  0.0 390.3 jit_solution(127312455419609033)
XLA Ops:
  6.5 0.7 fusion.13
  7.5 0.7 bitcast_subtract_fusion
  8.4 3.2 gather_fusion.2
  11.6 7.9 %all-to-all-start.1 = ((bf16[16,48,128]{2,1,0:T(8,128)(2,1)}), bf16[16,48,128]{2,1,0:T(8,128)(2,1)S(1)}, u32[]{:S(2)}, u32[]{:S(2)}) async-start(bf16[16,48,128]{2,1,0:T(8,128)(2,1)} %bitcast.28), calls=%async_computation.1 | async-start | bytes 393216 | tf_op jit(solution)/shard_map/all_to_all | solution.py:160
  19.5 3.3 gather_fusion
  22.8 5.1 %all-to-all-done.1 = bf16[16,48,128]{2,1,0:T(8,128)(2,1)S(1)} async-done(((bf16[16,48,128]{2,1,0:T(8,128)(2,1)}), bf16[16,48,128]{2,1,0:T(8,128)(2,1)S(1)}, u32[]{:S(2)}, u32[]{:S(2)}) %all-to-all-start.1) | async-done | bytes 196640 | tf_op jit(solution)/shard_map/all_to_all | solution.py:160
  27.8 3.6 all-to-all-start
  31.4 5.7 %fusion.19 = (bf16[512,2048]{1,0:T(8,128)(2,1)S(1)}, bf16[512,2048]{1,0:T(8,128)(2,1)}, bf16[512,2048]{1,0:T(8,128)(2,1)}, bf16[512,2048]{1,0:T(8,128)(2,1)}) fusion(bf16[512,8192]{1,0:T(8,128)(2,1)} %bitcast.129), kind=kLoop, calls=%fused_computation.70 | loop fusion | bytes 16777216 | tf_op jit(solution)/shard_map/slice | solution.py:221
  37.1 0.9 dynamic-slice_reduce_fusion
  38.1 9.0 %gather_fusion.4 = bf16[768,2048]{1,0:T(8,128)(2,1)} fusion(bf16[512,2048]{1,0:T(8,128)(2,1)} %get-tuple-element.19, s32[1024]{0:T(1024)S(1)} %pad_clamp_fusion.1), kind=kCustom, calls=%fused_computation.4 | custom fusion | bytes 6294528 | tf_op jit(solution)/shard_map/jit(_take)/gather | solution.py:159
  47.2 7.2 %all-to-all-start.2 = ((bf16[16,48,2048]{2,1,0:T(8,128)(2,1)}), bf16[16,48,2048]{2,1,0:T(8,128)(2,1)}, u32[]{:S(2)}, u32[]{:S(2)}) async-start(bf16[16,48,2048]{2,1,0:T(8,128)(2,1)} %bitcast.115), calls=%async_computation.2 | async-start | bytes 6291456 | tf_op jit(solution)/shard_map/all_to_all | solution.py:160
  54.5 0.7 fusion.21
  55.2 4.3 %compare_select_fusion.3 = (s32[512,1]{0,1:T(1,128)S(1)}, s32[512,1]{0,1:T(1,128)S(1)}) fusion(s32[]{:T(128)} %bitcast.17, s32[]{:T(128)} %bitcast.18, s32[]{:T(128)} %bitcast.19, s32[]{:T(128)} %bitcast.20, s32[]{:T(128)} %bitcast.21, s32[]{:T(128)} %bitcast.23, s32[]{:T(128)} %bitcast.22, s32[512,1]{0,1:T(1,128)S(1)} %bitcast.139), kind=kLoop, calls=%fused_computation.46 | loop fusion | flops 7680 | bytes 6172 | tf_op jit(solution)/shard_map/jit(_take)/gather | solution.py:188
  59.6 5.7 %select_select_fusion = s32[512]{0:T(512)S(1)} fusion(pred[512]{0:T(512)(128)(4,1)S(1)} %get-tuple-element.12, pred[512]{0:T(512)(128)(4,1)S(1)} %get-tuple-element.11, pred[512]{0:T(512)(128)(4,1)S(1)} %get-tuple-element.13, pred[512]{0:T(512)(128)(4,1)S(1)} %get-tuple-element.10, pred[512]{0:T(512)(128)(4,1)S(1)} %get-tuple-element.9, ...), kind=kLoop, calls=%fused_computation.59 | loop fusion | flops 4608 | bytes 8740 | tf_op jit(solution)/shard_map/jit(_take)/gather | solution.py:188
  65.4 1.3 gather_fusion.3
  66.8 0.9 compare_select_fusion.1
  68.8 2.7 copy.39
  71.5 0.7 reshape_reshape.7.decay_ref
  72.2 1.9 gather_fusion.1
  74.2 0.7 fusion.20
  74.8 0.7 copy.40
  75.6 21.1 %all-to-all-done.2 = bf16[16,48,2048]{2,1,0:T(8,128)(2,1)} async-done(((bf16[16,48,2048]{2,1,0:T(8,128)(2,1)}), bf16[16,48,2048]{2,1,0:T(8,128)(2,1)}, u32[]{:S(2)}, u32[]{:S(2)}) %all-to-all-start.2) | async-done | bytes 3145760 | tf_op jit(solution)/shard_map/all_to_all | solution.py:160
  96.7 7.5 %gather_fusion.5 = bf16[512,2048]{1,0:T(8,128)(2,1)} fusion(bf16[768,2048]{1,0:T(8,128)(2,1)} %bitcast.37, s32[1024]{0:T(1024)S(1)} %pad_clamp_fusion), kind=kCustom, calls=%fused_computation.5 | custom fusion | bytes 4196352 | tf_op jit(solution)/shard_map/jit(_take)/gather | solution.py:161
  104.2 5.7 %shard_map.65 = f32[16,136,128]{2,1,0:T(8,128)} custom-call(bf16[128,512]{1,0:T(8,128)(2,1)} %bitcast.131, f32[16,512,8]{2,1,0:T(8,128)} %bitcast.109, f32[1,8192]{1,0:T(1,128)} %reshape_reshape.7.decay_ref, bf16[512,2048]{1,0:T(8,128)(2,1)} %gather_fusion.5), custom_call_target="tpu_custom_call" | custom-call | tf_op jit(solution)/shard_map/pallas_call | solution.py:95
  110.0 0.3 all-gather.11.cloned.1.call-start
  110.3 9.0 %gather_fusion.6 = bf16[768,2048]{1,0:T(8,128)(2,1)} fusion(bf16[512,2048]{1,0:T(8,128)(2,1)} %get-tuple-element.18, s32[1024]{0:T(1024)S(1)} %pad_clamp_fusion.1), kind=kCustom, calls=%fused_computation.6 | custom fusion | bytes 6294528 | tf_op jit(solution)/shard_map/jit(_take)/gather | solution.py:159
  119.2 44.0 %all_to_all.30 = bf16[16,48,2048]{2,1,0:T(8,128)(2,1)} all-to-all(bf16[16,48,2048]{2,1,0:T(8,128)(2,1)} %bitcast.117), channel_id=1, replica_groups=mesh['pos'=8,'stream'=16] {'stream'}, dimensions={0} | all-to-all | bytes 6291456 | tf_op jit(solution)/shard_map/all_to_all | solution.py:160
  163.2 7.6 %gather_fusion.7 = bf16[512,2048]{1,0:T(8,128)(2,1)} fusion(bf16[768,2048]{1,0:T(8,128)(2,1)} %bitcast.107, s32[1024]{0:T(1024)S(1)} %pad_clamp_fusion), kind=kCustom, calls=%fused_computation.7 | custom fusion | bytes 4196352 | tf_op jit(solution)/shard_map/jit(_take)/gather | solution.py:161
  170.8 5.7 %shard_map.68 = f32[16,136,128]{2,1,0:T(8,128)} custom-call(bf16[128,512]{1,0:T(8,128)(2,1)} %bitcast.132, f32[16,512,8]{2,1,0:T(8,128)} %bitcast.110, f32[1,8192]{1,0:T(1,128)} %reshape_reshape.7.decay_ref, bf16[512,2048]{1,0:T(8,128)(2,1)} %gather_fusion.7), custom_call_target="tpu_custom_call" | custom-call | tf_op jit(solution)/shard_map/pallas_call | solution.py:95
  176.6 9.0 %gather_fusion.8 = bf16[768,2048]{1,0:T(8,128)(2,1)} fusion(bf16[512,2048]{1,0:T(8,128)(2,1)} %get-tuple-element.17, s32[1024]{0:T(1024)S(1)} %pad_clamp_fusion.1), kind=kCustom, calls=%fused_computation.8 | custom fusion | bytes 6294528 | tf_op jit(solution)/shard_map/jit(_take)/gather | solution.py:159
  185.5 42.6 %all_to_all.31 = bf16[16,48,2048]{2,1,0:T(8,128)(2,1)} all-to-all(bf16[16,48,2048]{2,1,0:T(8,128)(2,1)} %bitcast.118), channel_id=1, replica_groups=mesh['pos'=8,'stream'=16] {'stream'}, dimensions={0} | all-to-all | bytes 6291456 | tf_op jit(solution)/shard_map/all_to_all | solution.py:160
  228.2 7.5 %gather_fusion.9 = bf16[512,2048]{1,0:T(8,128)(2,1)} fusion(bf16[768,2048]{1,0:T(8,128)(2,1)} %bitcast.108, s32[1024]{0:T(1024)S(1)} %pad_clamp_fusion), kind=kCustom, calls=%fused_computation.9 | custom fusion | bytes 4196352 | tf_op jit(solution)/shard_map/jit(_take)/gather | solution.py:161
  235.7 5.7 %shard_map.71 = f32[16,136,128]{2,1,0:T(8,128)} custom-call(bf16[128,512]{1,0:T(8,128)(2,1)} %bitcast.133, f32[16,512,8]{2,1,0:T(8,128)} %bitcast.111, f32[1,8192]{1,0:T(1,128)} %reshape_reshape.7.decay_ref, bf16[512,2048]{1,0:T(8,128)(2,1)} %gather_fusion.9), custom_call_target="tpu_custom_call" | custom-call | tf_op jit(solution)/shard_map/pallas_call | solution.py:95
  241.5 4.3 %gather_fusion.10 = bf16[768,2048]{1,0:T(8,128)(2,1)} fusion(bf16[512,2048]{1,0:T(8,128)(2,1)S(1)} %get-tuple-element.16, s32[1024]{0:T(1024)S(1)} %pad_clamp_fusion.1), kind=kCustom, calls=%fused_computation.10 | custom fusion | bytes 6294528 | tf_op jit(solution)/shard_map/jit(_take)/gather | solution.py:159
  245.8 50.9 %all_to_all.32 = bf16[16,48,2048]{2,1,0:T(8,128)(2,1)} all-to-all(bf16[16,48,2048]{2,1,0:T(8,128)(2,1)} %bitcast.116), channel_id=1, replica_groups=mesh['pos'=8,'stream'=16] {'stream'}, dimensions={0} | all-to-all | bytes 6291456 | tf_op jit(solution)/shard_map/all_to_all | solution.py:160
  296.7 7.6 %gather_fusion.11 = bf16[512,2048]{1,0:T(8,128)(2,1)} fusion(bf16[768,2048]{1,0:T(8,128)(2,1)} %bitcast.106, s32[1024]{0:T(1024)S(1)} %pad_clamp_fusion), kind=kCustom, calls=%fused_computation.11 | custom fusion | bytes 4196352 | tf_op jit(solution)/shard_map/jit(_take)/gather | solution.py:161
  304.3 5.7 %shard_map.74 = f32[16,136,128]{2,1,0:T(8,128)} custom-call(bf16[128,512]{1,0:T(8,128)(2,1)} %bitcast.134, f32[16,512,8]{2,1,0:T(8,128)} %bitcast.112, f32[1,8192]{1,0:T(1,128)} %reshape_reshape.7.decay_ref, bf16[512,2048]{1,0:T(8,128)(2,1)} %gather_fusion.11), custom_call_target="tpu_custom_call" | custom-call | tf_op jit(solution)/shard_map/pallas_call | solution.py:95
  310.1 0.7 reshape_reshape.6.skip_ref
  310.8 2.6 copy.38
  313.4 1.3 fusion.14.scores_ref
  314.7 9.5 %shard_map.64.refs_0_ = f32[512,2048]{1,0:T(8,128)} custom-call(f32[512,512]{1,0:T(8,128)} %fusion.14.scores_ref, f32[16,512,8]{2,1,0:T(8,128)} %bitcast.98, f32[128,512]{1,0:T(8,128)} %bitcast.121, f32[128,512]{1,0:T(8,128)} %get-tuple-element.25.stept_ref, bf16[512,2048]{1,0:T(8,128)(2,1)} %gather_fusion.5, f32[1,8192]{1,0:T(1,128)} %reshape_reshape.6.skip_ref), custom_call_target="tpu_custom_call" | custom-call | tf_op jit(solution)/shard_map/pallas_call | solution.py:113
  324.2 9.5 %shard_map.67.refs_1_ = f32[512,2048]{1,0:T(8,128)} custom-call(f32[512,512]{1,0:T(8,128)} %fusion.14.scores_ref, f32[16,512,8]{2,1,0:T(8,128)} %bitcast.99, f32[128,512]{1,0:T(8,128)} %bitcast.122, f32[128,512]{1,0:T(8,128)} %get-tuple-element.25.stept_ref, bf16[512,2048]{1,0:T(8,128)(2,1)} %gather_fusion.7, f32[1,8192]{1,0:T(1,128)} %reshape_reshape.6.skip_ref), custom_call_target="tpu_custom_call" | custom-call | tf_op jit(solution)/shard_map/pallas_call | solution.py:113
  333.7 9.5 %shard_map.70.refs_1_ = f32[512,2048]{1,0:T(8,128)} custom-call(f32[512,512]{1,0:T(8,128)} %fusion.14.scores_ref, f32[16,512,8]{2,1,0:T(8,128)} %bitcast.100, f32[128,512]{1,0:T(8,128)} %bitcast.123, f32[128,512]{1,0:T(8,128)} %get-tuple-element.25.stept_ref, bf16[512,2048]{1,0:T(8,128)(2,1)} %gather_fusion.9, f32[1,8192]{1,0:T(1,128)} %reshape_reshape.6.skip_ref), custom_call_target="tpu_custom_call" | custom-call | tf_op jit(solution)/shard_map/pallas_call | solution.py:113
  343.2 9.5 %shard_map.73.refs_1_ = f32[512,2048]{1,0:T(8,128)} custom-call(f32[512,512]{1,0:T(8,128)} %fusion.14.scores_ref, f32[16,512,8]{2,1,0:T(8,128)} %bitcast.101, f32[128,512]{1,0:T(8,128)} %bitcast.124, f32[128,512]{1,0:T(8,128)} %get-tuple-element.25.stept_ref, bf16[512,2048]{1,0:T(8,128)(2,1)} %gather_fusion.11, f32[1,8192]{1,0:T(1,128)} %reshape_reshape.6.skip_ref), custom_call_target="tpu_custom_call" | custom-call | tf_op jit(solution)/shard_map/pallas_call | solution.py:113
  352.7 7.8 %shard_map.66.refs_0_ = bf16[512,8192]{1,0:T(8,128)(2,1)} custom-call(s32[1]{0:T(128)} %bitcast.place_ref, f32[512,2048]{1,0:T(8,128)} %shard_map.64.refs_0_, f32[8,16,136,128]{3,2,1,0:T(8,128)} %bitcast.128, f32[16,512,8]{2,1,0:T(8,128)} %bitcast.102, bf16[512,128]{1,0:T(8,128)(2,1)} %get-tuple-element.20.refs_3_.refs_4_), custom_call_target="tpu_custom_call" | custom-call | tf_op jit(solution)/shard_map/pallas_call | solution.py:146
  360.5 7.7 %shard_map.69.refs_0_ = bf16[512,8192]{1,0:T(8,128)(2,1)} custom-call(s32[1]{0:T(128)} %bitcast.place_ref, bf16[512,8192]{1,0:T(8,128)(2,1)} %shard_map.66.refs_0_, f32[512,2048]{1,0:T(8,128)} %shard_map.67.refs_1_, f32[8,16,136,128]{3,2,1,0:T(8,128)} %bitcast.125, f32[16,512,8]{2,1,0:T(8,128)} %bitcast.103, ...), custom_call_target="tpu_custom_call", output_to_operand_aliasing={{}: (1, {})} | custom-call | tf_op jit(solution)/shard_map/pallas_call | solution.py:146
  368.2 7.7 %shard_map.72.refs_0_ = bf16[512,8192]{1,0:T(8,128)(2,1)} custom-call(s32[1]{0:T(128)} %bitcast.place_ref, bf16[512,8192]{1,0:T(8,128)(2,1)} %shard_map.69.refs_0_, f32[512,2048]{1,0:T(8,128)} %shard_map.70.refs_1_, f32[8,16,136,128]{3,2,1,0:T(8,128)} %bitcast.126, f32[16,512,8]{2,1,0:T(8,128)} %bitcast.104, ...), custom_call_target="tpu_custom_call", output_to_operand_aliasing={{}: (1, {})} | custom-call | tf_op jit(solution)/shard_map/pallas_call | solution.py:146
  375.9 7.7 %shard_map.75 = bf16[512,8192]{1,0:T(8,128)(2,1)} custom-call(s32[1]{0:T(128)} %bitcast.place_ref, bf16[512,8192]{1,0:T(8,128)(2,1)} %shard_map.72.refs_0_, f32[512,2048]{1,0:T(8,128)} %shard_map.73.refs_1_, f32[8,16,136,128]{3,2,1,0:T(8,128)} %bitcast.127, f32[16,512,8]{2,1,0:T(8,128)} %bitcast.105, ...), custom_call_target="tpu_custom_call", output_to_operand_aliasing={{}: (1, {})} | custom-call | tf_op jit(solution)/shard_map/pallas_call | solution.py:146
  (53 shorter events, 2.2 us)
Async XLA Ops:
  6.5 12.9 %copy-start = (bf16[1,512,256]{2,1,0:T(8,128)(2,1)S(1)}, bf16[1,512,256]{2,1,0:T(8,128)(2,1)}, u32[]{:S(2)}) copy-start(bf16[1,512,256]{2,1,0:T(8,128)(2,1)} %param.7) | copy-start | bytes 786436
  11.6 16.2 %all-to-all-start.1 = ((bf16[16,48,128]{2,1,0:T(8,128)(2,1)}), bf16[16,48,128]{2,1,0:T(8,128)(2,1)S(1)}, u32[]{:S(2)}, u32[]{:S(2)}) async-start(bf16[16,48,128]{2,1,0:T(8,128)(2,1)} %bitcast.28), calls=%async_computation.1 | async-start | bytes 393216 | tf_op jit(solution)/shard_map/all_to_all | solution.py:160
  27.8 19.4 %all-to-all-start = ((bf16[16,48,256]{2,1,0:T(8,128)(2,1)}), bf16[16,48,256]{2,1,0:T(8,128)(2,1)S(1)}, u32[]{:S(2)}, u32[]{:S(2)}) async-start(bf16[16,48,256]{2,1,0:T(8,128)(2,1)} %bitcast.4), calls=%async_computation | async-start | bytes 786432 | tf_op jit(solution)/shard_map/all_to_all | solution.py:160
  47.2 18.1 %copy-start.4 = (f32[128]{0:T(128)S(1)}, f32[128]{0:T(128)}, u32[]{:S(2)}) copy-start(f32[128]{0:T(128)} %param.9) | copy-start | bytes 1540
  47.2 49.5 %all-to-all-start.2 = ((bf16[16,48,2048]{2,1,0:T(8,128)(2,1)}), bf16[16,48,2048]{2,1,0:T(8,128)(2,1)}, u32[]{:S(2)}, u32[]{:S(2)}) async-start(bf16[16,48,2048]{2,1,0:T(8,128)(2,1)} %bitcast.115), calls=%async_computation.2 | async-start | bytes 6291456 | tf_op jit(solution)/shard_map/all_to_all | solution.py:160
  54.4 298.3 %all-gather.9.cloned.1.call-start = ((), (), s32[]{:S(2)}) async-start(), calls=%async_computation.6 | async-start | bytes 10027008 | tf_op jit(solution)/shard_map/all_gather | solution.py:225
  68.4 242.5 %copy-start.2 = (f32[16,8,4,128]{3,1,2,0:T(8,128)}, f32[16,8,4,128]{3,1,2,0:T(8,128)S(1)}, u32[]{:S(2)}) copy-start(f32[16,8,4,128]{3,1,2,0:T(8,128)S(1)} %copy.49) | copy-start | bytes 786436
  110.0 250.5 %all-gather.11.cloned.1.call-start = ((), (), s32[]{:S(2)}) async-start(), calls=%async_computation.7 | async-start | bytes 10027008 | tf_op jit(solution)/shard_map/all_gather | solution.py:225
  176.5 191.7 %all-gather.13.cloned.1.call-start = ((), (), s32[]{:S(2)}) async-start(), calls=%async_computation.8 | async-start | bytes 10027008 | tf_op jit(solution)/shard_map/all_gather | solution.py:225
  241.4 134.5 %all-gather.15.cloned.1.call-start = ((), (), s32[]{:S(2)}) async-start(), calls=%async_computation.9 | async-start | bytes 10027008 | tf_op jit(solution)/shard_map/all_gather | solution.py:225
  304.3 5.7 %copy-start.3 = (f32[128]{0:T(128)S(1)}, f32[128]{0:T(128)}, u32[]{:S(2)}) copy-start(f32[128]{0:T(128)} %param.10) | copy-start | bytes 1540
  375.9 7.7 %copy-start.1 = (bf16[1,512,256]{2,1,0:T(8,128)(2,1)S(1)}, bf16[1,512,256]{2,1,0:T(8,128)(2,1)}, u32[]{:S(2)}) copy-start(bf16[1,512,256]{2,1,0:T(8,128)(2,1)} %param.7) | copy-start | bytes 786436
Sparse Core Ops, SparseCore 0:
  110.1 47.9 all-gather.8
  176.7 47.5 all-gather.10
  241.5 47.0 all-gather.12
  310.1 47.1 all-gather.14

commit v3 on v2

--- a/solution.py
+++ b/solution.py
@@ -154,10 +154,12 @@
     )(place, *operands)
 
 
-def deliver(rows, pick_rows, flat_rows, stream_count, capacity):
+def deliver(rows, pick_rows, flat_rows, stream_count, capacity, previous=None):
     width = rows.shape[1]
     send = jnp.take(rows, pick_rows, axis=0, mode="clip").reshape(stream_count, capacity, width)
     arrived = lax.all_to_all(send, "stream", split_axis=0, concat_axis=0, tiled=True)
+    if previous is not None:
+        arrived, _ = lax.optimization_barrier((arrived, previous))
     return jnp.take(
         arrived.reshape(stream_count * capacity, width), flat_rows, axis=0, mode="clip"
     )
@@ -188,8 +190,10 @@
     source_start = jnp.take(recv_start, source)
     flat_rows = source * capacity + positions - source_start
 
-    ordered_proj = deliver(proj_in[0], pick_rows, flat_rows, stream_count, capacity)
-    ordered_steps = deliver(step_raw[0], pick_rows, flat_rows, stream_count, capacity)
+    small = jnp.concatenate([proj_in[0], step_raw[0]], axis=1)
+    ordered_small = deliver(small, pick_rows, flat_rows, stream_count, capacity)
+    ordered_proj = ordered_small[:, : 2 * state_size]
+    ordered_steps = ordered_small[:, 2 * state_size :]
 
     inputs = ordered_proj[:, :state_size]
     readout = ordered_proj[:, state_size:]
@@ -216,15 +220,18 @@
     width = inner // CHUNKS
     groups_per_chunk = groups // CHUNKS
     pieces = []
+    previous = None
     for c in range(CHUNKS):
         chunk_tokens = deliver(
-            tokens[:, c * width : (c + 1) * width], pick_rows, flat_rows, stream_count, capacity
+            tokens[:, c * width : (c + 1) * width], pick_rows, flat_rows, stream_count, capacity,
+            previous,
         )
         first = c * groups_per_chunk
         carried = carried_call(bt, fac_grouped, decay_lanes, chunk_tokens, first)
         gathered = lax.all_gather(carried, "pos")
         partial = local_call(scores, cum_grouped, cum_t, step_t, chunk_tokens, skip_lanes, first)
         pieces.append((partial, gathered, first))
+        previous = partial
     result = None
     for partial, gathered, first in pieces:
         result = combine_call(

time: 395 us -> 379 us (0.959)
  the two profiles are of different devices: /device:TPU:24 before, /device:TPU:1 now
where the time goes in v3:
time: 379 us; the launch traced here: 374 us
  waiting for transfers between devices  136 us (36%)
  Pallas kernels  92.8 us (24%)
  local copies, waits for them, and re-layouts  84.8 us (22%)
  starting transfers between devices  32.4 us (9%)
  between operations  13.6 us (4%)
  other arithmetic  13.5 us (4%)
    all_to_all x5, waiting for transfers between devices, deliver(): lax.all_to_all(send, 'stream', split_axis=0, concat_axis=0, tiled=True)  116 us
    pallas_call x4, Pallas kernels, local_call(): pl.pallas_call(local_kernel, grid=(groups,), in_specs=[pl.BlockSpec((leng...  38.1 us
    gather x5, local copies, waits for them, and re-layouts, deliver(): jnp.take(rows, pick_rows, axis=0, mode='clip')  34.5 us
    gather x5, local copies, waits for them, and re-layouts, deliver(): jnp.take(arrived.reshape(stream_count * capacity, width), flat_rows, axis...  32.1 us
    pallas_call x4, Pallas kernels, combine_call(): pl.pallas_call(combine_kernel, grid=(groups,), in_specs=[pl.BlockSpec(mem...  31.9 us
    all_to_all x5, starting transfers between devices, deliver(): lax.all_to_all(send, 'stream', split_axis=0, concat_axis=0, tiled=True)  31.1 us
    pallas_call x4, Pallas kernels, carried_call(): pl.pallas_call(carried_kernel, grid=(groups,), in_specs=[pl.BlockSpec(bt....  22.8 us
    all_gather x4, waiting for transfers between devices, on_device(): gathered = lax.all_gather(carried, 'pos')  19.9 us
  transfers between devices with their start and end apart: 9, of which 5 were waited for; matrix products, arithmetic and copies ran while one was open for 23% of the time, Pallas kernels for 21%

profile of v3, /device:TPU:1, one launch (start us, length us, event | category | flops | bytes accessed | tf_op | source)
XLA Modules:
  0.0 374.1 jit_solution(10584187966806164138)
XLA Ops:
  6.5 0.7 fusion.6
  7.5 0.7 bitcast_subtract_fusion
  8.3 1.1 pad_maximum_fusion
  9.4 3.2 gather_fusion
  12.6 8.4 %all-to-all-start = ((bf16[16,48,384]{2,1,0:T(8,128)(2,1)}), bf16[16,48,384]{2,1,0:T(8,128)(2,1)S(1)}, u32[]{:S(2)}, u32[]{:S(2)}) async-start(bf16[16,48,384]{2,1,0:T(8,128)(2,1)} %bitcast.5), calls=%async_computation | async-start | bytes 1179648 | tf_op jit(solution)/shard_map/all_to_all | solution.py:160
  21.1 0.9 dynamic-slice_reduce_fusion
  22.1 5.7 %fusion.12 = (bf16[512,2048]{1,0:T(8,128)(2,1)S(1)}, bf16[512,2048]{1,0:T(8,128)(2,1)}, bf16[512,2048]{1,0:T(8,128)(2,1)}, bf16[512,2048]{1,0:T(8,128)(2,1)}) fusion(bf16[512,8192]{1,0:T(8,128)(2,1)} %bitcast.104), kind=kLoop, calls=%fused_computation.61 | loop fusion | bytes 16777216 | tf_op jit(solution)/shard_map/slice | solution.py:226
  27.8 9.0 %gather_fusion.2 = bf16[768,2048]{1,0:T(8,128)(2,1)} fusion(bf16[512,2048]{1,0:T(8,128)(2,1)} %get-tuple-element.25, s32[1024]{0:T(1024)S(1)} %pad_clamp_fusion.1), kind=kCustom, calls=%fused_computation.2 | custom fusion | bytes 6294528 | tf_op jit(solution)/shard_map/jit(_take)/gather | solution.py:159
  36.9 6.7 %all-to-all-start.1 = ((bf16[16,48,2048]{2,1,0:T(8,128)(2,1)}), bf16[16,48,2048]{2,1,0:T(8,128)(2,1)}, u32[]{:S(2)}, u32[]{:S(2)}) async-start(bf16[16,48,2048]{2,1,0:T(8,128)(2,1)} %bitcast.90), calls=%async_computation.1 | async-start | bytes 6291456 | tf_op jit(solution)/shard_map/all_to_all | solution.py:160
  44.0 0.7 fusion.14
  44.7 4.3 %compare_select_fusion.2 = (s32[512,1]{0,1:T(1,128)S(1)}, s32[512,1]{0,1:T(1,128)S(1)}) fusion(s32[]{:T(128)} %bitcast.18, s32[]{:T(128)} %bitcast.19, s32[]{:T(128)} %bitcast.20, s32[]{:T(128)} %bitcast.21, s32[]{:T(128)} %bitcast.22, s32[]{:T(128)} %bitcast.24, s32[]{:T(128)} %bitcast.23, s32[512,1]{0,1:T(1,128)S(1)} %bitcast.115), kind=kLoop, calls=%fused_computation.37 | loop fusion | flops 7680 | bytes 6172 | tf_op jit(solution)/shard_map/jit(_take)/gather | solution.py:190
  49.1 5.6 %select_select_fusion = s32[512]{0:T(512)S(1)} fusion(pred[512]{0:T(512)(128)(4,1)S(1)} %get-tuple-element.18, pred[512]{0:T(512)(128)(4,1)S(1)} %get-tuple-element.17, pred[512]{0:T(512)(128)(4,1)S(1)} %get-tuple-element.19, pred[512]{0:T(512)(128)(4,1)S(1)} %get-tuple-element.16, pred[512]{0:T(512)(128)(4,1)S(1)} %get-tuple-element.15, ...), kind=kLoop, calls=%fused_computation.50 | loop fusion | flops 4608 | bytes 8740 | tf_op jit(solution)/shard_map/jit(_take)/gather | solution.py:190
  54.8 1.9 gather_fusion.1
  56.7 0.8 fusion.13
  58.4 1.7 copy.40
  60.4 0.9 multiply_bitcast_fusion
  61.3 2.7 copy.39
  64.0 0.7 reshape_reshape.7.decay_ref
  64.7 24.0 %all-to-all-done.1 = bf16[16,48,2048]{2,1,0:T(8,128)(2,1)} async-done(((bf16[16,48,2048]{2,1,0:T(8,128)(2,1)}), bf16[16,48,2048]{2,1,0:T(8,128)(2,1)}, u32[]{:S(2)}, u32[]{:S(2)}) %all-to-all-start.1) | async-done | bytes 3145760 | tf_op jit(solution)/shard_map/all_to_all | solution.py:160
  88.7 7.5 %gather_fusion.3 = bf16[512,2048]{1,0:T(8,128)(2,1)} fusion(bf16[768,2048]{1,0:T(8,128)(2,1)} %bitcast.36, s32[1024]{0:T(1024)S(1)} %pad_clamp_fusion), kind=kCustom, calls=%fused_computation.3 | custom fusion | bytes 4196352 | tf_op jit(solution)/shard_map/jit(_take)/gather | solution.py:163
  96.3 5.7 %shard_map.65 = f32[16,136,128]{2,1,0:T(8,128)} custom-call(bf16[128,512]{1,0:T(8,128)(2,1)} %bitcast.105, f32[16,512,8]{2,1,0:T(8,128)} %bitcast.85, f32[1,8192]{1,0:T(1,128)} %reshape_reshape.7.decay_ref, bf16[512,2048]{1,0:T(8,128)(2,1)} %gather_fusion.3), custom_call_target="tpu_custom_call" | custom-call | tf_op jit(solution)/shard_map/pallas_call | solution.py:95
  102.0 9.0 %gather_fusion.4 = bf16[768,2048]{1,0:T(8,128)(2,1)} fusion(bf16[512,2048]{1,0:T(8,128)(2,1)} %get-tuple-element.24, s32[1024]{0:T(1024)S(1)} %pad_clamp_fusion.1), kind=kCustom, calls=%fused_computation.4 | custom fusion | bytes 6294528 | tf_op jit(solution)/shard_map/jit(_take)/gather | solution.py:159
  110.9 4.7 %all-to-all-start.2 = ((bf16[16,48,2048]{2,1,0:T(8,128)(2,1)}), bf16[16,48,2048]{2,1,0:T(8,128)(2,1)}, u32[]{:S(2)}, u32[]{:S(2)}) async-start(bf16[16,48,2048]{2,1,0:T(8,128)(2,1)} %bitcast.91), calls=%async_computation.2 | async-start | bytes 6291456 | tf_op jit(solution)/shard_map/all_to_all | solution.py:160
  116.3 0.7 reshape_reshape.6.skip_ref
  117.0 2.6 copy.38
  119.6 1.3 fusion.7.scores_ref
  120.9 9.4 %shard_map.64.refs_0_ = f32[512,2048]{1,0:T(8,128)} custom-call(f32[512,512]{1,0:T(8,128)} %fusion.7.scores_ref, f32[16,512,8]{2,1,0:T(8,128)} %bitcast.77, f32[128,512]{1,0:T(8,128)} %bitcast.96, f32[128,512]{1,0:T(8,128)} %get-tuple-element.33.stept_ref, bf16[512,2048]{1,0:T(8,128)(2,1)} %gather_fusion.3, f32[1,8192]{1,0:T(1,128)} %reshape_reshape.6.skip_ref), custom_call_target="tpu_custom_call" | custom-call | tf_op jit(solution)/shard_map/pallas_call | solution.py:113
  130.4 27.5 %all-to-all-done.2 = bf16[16,48,2048]{2,1,0:T(8,128)(2,1)} async-done(((bf16[16,48,2048]{2,1,0:T(8,128)(2,1)}), bf16[16,48,2048]{2,1,0:T(8,128)(2,1)}, u32[]{:S(2)}, u32[]{:S(2)}) %all-to-all-start.2) | async-done | bytes 3145760 | tf_op jit(solution)/shard_map/all_to_all | solution.py:160
  157.9 7.6 %gather_fusion.5 = bf16[512,2048]{1,0:T(8,128)(2,1)} fusion(bf16[768,2048]{1,0:T(8,128)(2,1)} %bitcast.42, s32[1024]{0:T(1024)S(1)} %pad_clamp_fusion), kind=kCustom, calls=%fused_computation.5 | custom fusion | bytes 4196352 | tf_op jit(solution)/shard_map/jit(_take)/gather | solution.py:163
  165.5 5.7 %shard_map.68 = f32[16,136,128]{2,1,0:T(8,128)} custom-call(bf16[128,512]{1,0:T(8,128)(2,1)} %bitcast.106, f32[16,512,8]{2,1,0:T(8,128)} %bitcast.86, f32[1,8192]{1,0:T(1,128)} %reshape_reshape.7.decay_ref, bf16[512,2048]{1,0:T(8,128)(2,1)} %gather_fusion.5), custom_call_target="tpu_custom_call" | custom-call | tf_op jit(solution)/shard_map/pallas_call | solution.py:95
  171.2 9.0 %gather_fusion.6 = bf16[768,2048]{1,0:T(8,128)(2,1)} fusion(bf16[512,2048]{1,0:T(8,128)(2,1)} %get-tuple-element.23, s32[1024]{0:T(1024)S(1)} %pad_clamp_fusion.1), kind=kCustom, calls=%fused_computation.6 | custom fusion | bytes 6294528 | tf_op jit(solution)/shard_map/jit(_take)/gather | solution.py:159
  180.2 5.4 %all-to-all-start.3 = ((bf16[16,48,2048]{2,1,0:T(8,128)(2,1)}), bf16[16,48,2048]{2,1,0:T(8,128)(2,1)}, u32[]{:S(2)}, u32[]{:S(2)}) async-start(bf16[16,48,2048]{2,1,0:T(8,128)(2,1)} %bitcast.93), calls=%async_computation.3 | async-start | bytes 6291456 | tf_op jit(solution)/shard_map/all_to_all | solution.py:160
  185.9 9.5 %shard_map.67.refs_1_ = f32[512,2048]{1,0:T(8,128)} custom-call(f32[512,512]{1,0:T(8,128)} %fusion.7.scores_ref, f32[16,512,8]{2,1,0:T(8,128)} %bitcast.78, f32[128,512]{1,0:T(8,128)} %bitcast.97, f32[128,512]{1,0:T(8,128)} %get-tuple-element.33.stept_ref, bf16[512,2048]{1,0:T(8,128)(2,1)} %gather_fusion.5, f32[1,8192]{1,0:T(1,128)} %reshape_reshape.6.skip_ref), custom_call_target="tpu_custom_call" | custom-call | tf_op jit(solution)/shard_map/pallas_call | solution.py:113
  195.3 32.0 %all-to-all-done.3 = bf16[16,48,2048]{2,1,0:T(8,128)(2,1)} async-done(((bf16[16,48,2048]{2,1,0:T(8,128)(2,1)}), bf16[16,48,2048]{2,1,0:T(8,128)(2,1)}, u32[]{:S(2)}, u32[]{:S(2)}) %all-to-all-start.3) | async-done | bytes 3145760 | tf_op jit(solution)/shard_map/all_to_all | solution.py:160
  227.3 7.5 %gather_fusion.7 = bf16[512,2048]{1,0:T(8,128)(2,1)} fusion(bf16[768,2048]{1,0:T(8,128)(2,1)} %bitcast.45, s32[1024]{0:T(1024)S(1)} %pad_clamp_fusion), kind=kCustom, calls=%fused_computation.7 | custom fusion | bytes 4196352 | tf_op jit(solution)/shard_map/jit(_take)/gather | solution.py:163
  234.8 5.7 %shard_map.71 = f32[16,136,128]{2,1,0:T(8,128)} custom-call(bf16[128,512]{1,0:T(8,128)(2,1)} %bitcast.107, f32[16,512,8]{2,1,0:T(8,128)} %bitcast.87, f32[1,8192]{1,0:T(1,128)} %reshape_reshape.7.decay_ref, bf16[512,2048]{1,0:T(8,128)(2,1)} %gather_fusion.7), custom_call_target="tpu_custom_call" | custom-call | tf_op jit(solution)/shard_map/pallas_call | solution.py:95
  240.6 4.3 %gather_fusion.8 = bf16[768,2048]{1,0:T(8,128)(2,1)} fusion(bf16[512,2048]{1,0:T(8,128)(2,1)S(1)} %get-tuple-element.22, s32[1024]{0:T(1024)S(1)} %pad_clamp_fusion.1), kind=kCustom, calls=%fused_computation.8 | custom fusion | bytes 6294528 | tf_op jit(solution)/shard_map/jit(_take)/gather | solution.py:159
  244.9 5.8 %all-to-all-start.4 = ((bf16[16,48,2048]{2,1,0:T(8,128)(2,1)}), bf16[16,48,2048]{2,1,0:T(8,128)(2,1)}, u32[]{:S(2)}, u32[]{:S(2)}) async-start(bf16[16,48,2048]{2,1,0:T(8,128)(2,1)} %bitcast.92), calls=%async_computation.4 | async-start | bytes 6291456 | tf_op jit(solution)/shard_map/all_to_all | solution.py:160
  250.9 9.7 %shard_map.70.refs_1_ = f32[512,2048]{1,0:T(8,128)} custom-call(f32[512,512]{1,0:T(8,128)} %fusion.7.scores_ref, f32[16,512,8]{2,1,0:T(8,128)} %bitcast.79, f32[128,512]{1,0:T(8,128)} %bitcast.98, f32[128,512]{1,0:T(8,128)} %get-tuple-element.33.stept_ref, bf16[512,2048]{1,0:T(8,128)(2,1)} %gather_fusion.7, f32[1,8192]{1,0:T(1,128)} %reshape_reshape.6.skip_ref), custom_call_target="tpu_custom_call" | custom-call | tf_op jit(solution)/shard_map/pallas_call | solution.py:113
  260.7 32.2 %all-to-all-done.4 = bf16[16,48,2048]{2,1,0:T(8,128)(2,1)} async-done(((bf16[16,48,2048]{2,1,0:T(8,128)(2,1)}), bf16[16,48,2048]{2,1,0:T(8,128)(2,1)}, u32[]{:S(2)}, u32[]{:S(2)}) %all-to-all-start.4) | async-done | bytes 3145760 | tf_op jit(solution)/shard_map/all_to_all | solution.py:160
  292.9 7.5 %gather_fusion.9 = bf16[512,2048]{1,0:T(8,128)(2,1)} fusion(bf16[768,2048]{1,0:T(8,128)(2,1)} %bitcast.48, s32[1024]{0:T(1024)S(1)} %pad_clamp_fusion), kind=kCustom, calls=%fused_computation.9 | custom fusion | bytes 4196352 | tf_op jit(solution)/shard_map/jit(_take)/gather | solution.py:163
  300.4 5.7 %shard_map.74 = f32[16,136,128]{2,1,0:T(8,128)} custom-call(bf16[128,512]{1,0:T(8,128)(2,1)} %bitcast.108, f32[16,512,8]{2,1,0:T(8,128)} %bitcast.88, f32[1,8192]{1,0:T(1,128)} %reshape_reshape.7.decay_ref, bf16[512,2048]{1,0:T(8,128)(2,1)} %gather_fusion.9), custom_call_target="tpu_custom_call" | custom-call | tf_op jit(solution)/shard_map/pallas_call | solution.py:95
  306.1 9.5 %shard_map.73.refs_1_ = f32[512,2048]{1,0:T(8,128)} custom-call(f32[512,512]{1,0:T(8,128)} %fusion.7.scores_ref, f32[16,512,8]{2,1,0:T(8,128)} %bitcast.80, f32[128,512]{1,0:T(8,128)} %bitcast.99, f32[128,512]{1,0:T(8,128)} %get-tuple-element.33.stept_ref, bf16[512,2048]{1,0:T(8,128)(2,1)} %gather_fusion.9, f32[1,8192]{1,0:T(1,128)} %reshape_reshape.6.skip_ref), custom_call_target="tpu_custom_call" | custom-call | tf_op jit(solution)/shard_map/pallas_call | solution.py:113
  315.5 8.5 %shard_map.66.refs_0_ = bf16[512,8192]{1,0:T(8,128)(2,1)} custom-call(s32[1]{0:T(128)} %bitcast.place_ref, f32[512,2048]{1,0:T(8,128)} %shard_map.64.refs_0_, f32[8,16,136,128]{3,2,1,0:T(8,128)} %bitcast.103, f32[16,512,8]{2,1,0:T(8,128)} %bitcast.81, bf16[512,128]{1,0:T(8,128)(2,1)} %get-tuple-element.26.refs_3_.refs_4_), custom_call_target="tpu_custom_call" | custom-call | tf_op jit(solution)/shard_map/pallas_call | solution.py:146
  324.0 7.9 %shard_map.69.refs_0_ = bf16[512,8192]{1,0:T(8,128)(2,1)} custom-call(s32[1]{0:T(128)} %bitcast.place_ref, bf16[512,8192]{1,0:T(8,128)(2,1)} %shard_map.66.refs_0_, f32[512,2048]{1,0:T(8,128)} %shard_map.67.refs_1_, f32[8,16,136,128]{3,2,1,0:T(8,128)} %bitcast.100, f32[16,512,8]{2,1,0:T(8,128)} %bitcast.82, ...), custom_call_target="tpu_custom_call", output_to_operand_aliasing={{}: (1, {})} | custom-call | tf_op jit(solution)/shard_map/pallas_call | solution.py:146
  331.9 7.9 %shard_map.72.refs_0_ = bf16[512,8192]{1,0:T(8,128)(2,1)} custom-call(s32[1]{0:T(128)} %bitcast.place_ref, bf16[512,8192]{1,0:T(8,128)(2,1)} %shard_map.69.refs_0_, f32[512,2048]{1,0:T(8,128)} %shard_map.70.refs_1_, f32[8,16,136,128]{3,2,1,0:T(8,128)} %bitcast.101, f32[16,512,8]{2,1,0:T(8,128)} %bitcast.83, ...), custom_call_target="tpu_custom_call", output_to_operand_aliasing={{}: (1, {})} | custom-call | tf_op jit(solution)/shard_map/pallas_call | solution.py:146
  339.8 19.9 %all-gather.15.cloned.1.call-done = f32[128,136,128]{2,1,0:T(8,128)} async-done(((f32[16,136,128]{2,1,0:T(8,128)}), f32[128,136,128]{2,1,0:T(8,128)}) %all-gather.15.cloned.1.call-update) | async-done | bytes 8912912 | tf_op jit(solution)/shard_map/all_gather | solution.py:231
  359.7 7.7 %shard_map.75 = bf16[512,8192]{1,0:T(8,128)(2,1)} custom-call(s32[1]{0:T(128)} %bitcast.place_ref, bf16[512,8192]{1,0:T(8,128)(2,1)} %shard_map.72.refs_0_, f32[512,2048]{1,0:T(8,128)} %shard_map.73.refs_1_, f32[8,16,136,128]{3,2,1,0:T(8,128)} %bitcast.102, f32[16,512,8]{2,1,0:T(8,128)} %bitcast.84, ...), custom_call_target="tpu_custom_call", output_to_operand_aliasing={{}: (1, {})} | custom-call | tf_op jit(solution)/shard_map/pallas_call | solution.py:146
  (49 shorter events, 3.4 us)
Async XLA Ops:
  12.6 24.3 %all-to-all-start = ((bf16[16,48,384]{2,1,0:T(8,128)(2,1)}), bf16[16,48,384]{2,1,0:T(8,128)(2,1)S(1)}, u32[]{:S(2)}, u32[]{:S(2)}) async-start(bf16[16,48,384]{2,1,0:T(8,128)(2,1)} %bitcast.5), calls=%async_computation | async-start | bytes 1179648 | tf_op jit(solution)/shard_map/all_to_all | solution.py:160
  36.9 17.8 %copy-start.2 = (f32[128]{0:T(128)S(1)}, f32[128]{0:T(128)}, u32[]{:S(2)}) copy-start(f32[128]{0:T(128)} %param.9) | copy-start | bytes 1540
  36.9 51.8 %all-to-all-start.1 = ((bf16[16,48,2048]{2,1,0:T(8,128)(2,1)}), bf16[16,48,2048]{2,1,0:T(8,128)(2,1)}, u32[]{:S(2)}, u32[]{:S(2)}) async-start(bf16[16,48,2048]{2,1,0:T(8,128)(2,1)} %bitcast.90), calls=%async_computation.1 | async-start | bytes 6291456 | tf_op jit(solution)/shard_map/all_to_all | solution.py:160
  43.6 271.9 %all-gather.9.cloned.1.call-start = ((), (), s32[]{:S(2)}) async-start(), calls=%async_computation.5 | async-start | bytes 10027008 | tf_op jit(solution)/shard_map/all_gather | solution.py:231
  58.4 58.6 %copy-start = (f32[16,8,4,128]{3,1,2,0:T(8,128)}, f32[16,8,4,128]{3,1,2,0:T(8,128)S(1)}, u32[]{:S(2)}) copy-start(f32[16,8,4,128]{3,1,2,0:T(8,128)S(1)} %copy.50) | copy-start | bytes 786436
  110.9 5.3 %copy-start.1 = (f32[128]{0:T(128)S(1)}, f32[128]{0:T(128)}, u32[]{:S(2)}) copy-start(f32[128]{0:T(128)} %param.10) | copy-start | bytes 1540
  110.9 47.0 %all-to-all-start.2 = ((bf16[16,48,2048]{2,1,0:T(8,128)(2,1)}), bf16[16,48,2048]{2,1,0:T(8,128)(2,1)}, u32[]{:S(2)}, u32[]{:S(2)}) async-start(bf16[16,48,2048]{2,1,0:T(8,128)(2,1)} %bitcast.91), calls=%async_computation.2 | async-start | bytes 6291456 | tf_op jit(solution)/shard_map/all_to_all | solution.py:160
  115.7 208.4 %all-gather.11.cloned.1.call-start = ((), (), s32[]{:S(2)}) async-start(), calls=%async_computation.6 | async-start | bytes 10027008 | tf_op jit(solution)/shard_map/all_gather | solution.py:231
  180.2 47.1 %all-to-all-start.3 = ((bf16[16,48,2048]{2,1,0:T(8,128)(2,1)}), bf16[16,48,2048]{2,1,0:T(8,128)(2,1)}, u32[]{:S(2)}, u32[]{:S(2)}) async-start(bf16[16,48,2048]{2,1,0:T(8,128)(2,1)} %bitcast.93), calls=%async_computation.3 | async-start | bytes 6291456 | tf_op jit(solution)/shard_map/all_to_all | solution.py:160
  185.7 146.3 %all-gather.13.cloned.1.call-start = ((), (), s32[]{:S(2)}) async-start(), calls=%async_computation.7 | async-start | bytes 10027008 | tf_op jit(solution)/shard_map/all_gather | solution.py:231
  244.9 48.0 %all-to-all-start.4 = ((bf16[16,48,2048]{2,1,0:T(8,128)(2,1)}), bf16[16,48,2048]{2,1,0:T(8,128)(2,1)}, u32[]{:S(2)}, u32[]{:S(2)}) async-start(bf16[16,48,2048]{2,1,0:T(8,128)(2,1)} %bitcast.92), calls=%async_computation.4 | async-start | bytes 6291456 | tf_op jit(solution)/shard_map/all_to_all | solution.py:160
  250.7 109.0 %all-gather.15.cloned.1.call-start = ((), (), s32[]{:S(2)}) async-start(), calls=%async_computation.8 | async-start | bytes 10027008 | tf_op jit(solution)/shard_map/all_gather | solution.py:231
Sparse Core Ops, SparseCore 0:
  102.1 51.8 all-gather.8
  171.4 53.2 all-gather.10
  240.7 53.6 all-gather.12
  306.2 53.4 all-gather.14
